TPU v7x, 32 devices: a whole 2x2x4 slice. The times are simulated.
32 devices in a mesh: parts: 2 (over y), filt: 4 (over z), space: 4 (over x, core).
Axes of the slice: x: 2, y: 2, z: 4, core: 2. Of those that a mesh axis runs over, the one named last changes fastest.
Arguments:
- volume: bfloat16 [512, 16, 8, 128], P('filt', ('parts', 'space')), parts along dimension 1, may hold values from -6 to 6
- weight: bfloat16 [512, 27, 512], P('filt'), may hold values from -0.0546875 to 0.0546875
- bias: float32 [512], P('filt'), may hold values from -3 to 3
- upstream: bfloat16 [512, 16, 8, 128], P('filt', ('parts', 'space')), parts along dimension 1, may hold values from -0.0625 to 0.0625
Outputs:
- features: bfloat16 [512, 16, 8, 128], P('filt', ('parts', 'space')), parts along dimension 1
- weight_grad: float32 [1024, 27, 512], P(('parts', 'filt')), parts along dimension 0
There are 2 independent parts, one for each index of `parts`. A program takes and returns all parts, laid end to end along the dimension named above; an argument that names none is the same for every part. Nothing has to cross between parts.
All inputs are finite; a program needn't handle non-finite values.
Results may differ from a plain program's by a relative error of at most 0.001.
Values may be sent and summed in bfloat16 or wider, within the bound.
No kernel may reach another device: no remote copies, remote signals or barrier semaphores. Data moves between devices by JAX's collectives and lax.ppermute only.
A program may use at most 128 MiB of HBM per device.

v0:
```python
import jax
import jax.numpy as jnp
from jax import lax
from jax.sharding import PartitionSpec as P


def padded(block, sides, width):
    for axis, dim in sides:
        count = lax.axis_size(axis)
        forward = [(i, i + 1) for i in range(count - 1)]
        backward = [(target, source) for source, target in forward]
        low = lax.ppermute(
            lax.slice_in_dim(block, block.shape[dim] - width, None, axis=dim), axis, forward
        )
        high = lax.ppermute(lax.slice_in_dim(block, 0, width, axis=dim), axis, backward)
        block = jnp.concatenate([low, block, high], axis=dim)
    return block


def convolve(slab, kernel):
    return lax.conv_general_dilated(
        slab[None],
        kernel,
        (1, 1, 1),
        [(0, 0), (1, 1), (1, 1)],
        dimension_numbers=("NCDHW", "OIDHW", "NCDHW"),
        preferred_element_type=jnp.float32,
    )[0]


def shifted_slopes(upstream):
    out_dev = upstream.shape[0]
    depth = upstream.shape[1]
    height = upstream.shape[2]
    length = upstream.shape[3]
    spread = jnp.pad(upstream, ((0, 0), (2, 2), (1, 1), (1, 1)))
    copies = []
    for tap in range(27):
        first = tap // 9
        second = tap // 3 % 3
        third = tap % 3
        copies.append(
            spread[
                :,
                2 - first : 4 - first + depth,
                2 - second : 2 - second + height,
                2 - third : 2 - third + length,
            ]
        )
    stacked = jnp.stack(copies, 1)
    return stacked.reshape(out_dev * 27, (depth + 2) * height * length)


def tap_grads(slab, slopes, out_dev):
    flat = slab.reshape(slab.shape[0], -1)
    product = lax.dot_general(
        slopes, flat, (((1,), (1,)), ((), ())), preferred_element_type=jnp.float32
    )
    return product.reshape(out_dev, 27, slab.shape[0])


def on_device(volume, weight, bias, upstream):
    out_dev = weight.shape[0]
    in_all = weight.shape[2]
    kernel = weight.reshape(out_dev, 3, 3, 3, in_all).transpose(0, 4, 1, 2, 3)
    slopes = shifted_slopes(upstream)
    whole = lax.all_gather(volume, "filt", axis=0, tiled=True)
    rimmed = padded(whole, (("space", 1),), 1)
    pre = convolve(rimmed, kernel)
    partial_grads = tap_grads(rimmed, slopes, out_dev)
    weight_grad = lax.psum(partial_grads, "space")
    pre = pre + bias[:, None, None, None]
    features = jnp.where(pre > 0, pre, 0.3 * pre).astype(jnp.bfloat16)
    return (features, weight_grad)


def solution(mesh):
    return jax.shard_map(
        on_device,
        mesh=mesh,
        in_specs=(
            P("filt", ("parts", "space"), None, None),
            P("filt", None, None),
            P("filt"),
            P("filt", ("parts", "space"), None, None),
        ),
        out_specs=(P("filt", ("parts", "space"), None, None), P(("parts", "filt"), None, None)),
        check_vma=False,
    )
```

profile of v0, /device:TPU:0, one launch (start us, length us, event | category | flops | bytes accessed | tf_op | source)
XLA Modules:
  0.0 254.6 jit_solution(8644923369791404062)
XLA Ops:
  7.2 2.1 copy.8
  20.5 1.4 fusion.35
  25.6 1.4 fusion.43
  34.4 24.5 %all-gather.2.cloned.1.call-done = bf16[512,2,8,128]{3,0,2,1:T(8,128)(2,1)} async-done(((bf16[128,2,8,128]{3,0,2,1:T(8,128)(2,1)}), bf16[512,2,8,128]{3,0,2,1:T(8,128)(2,1)}) %all-gather.2.cloned.1.call-update) | async-done | bytes 2097168 | tf_op jit(solution)/shard_map/all_gather | solution.py:67
  58.8 1.7 fusion.76
  60.5 1.8 collective-permute-start
  62.3 2.2 fusion.57
  64.5 2.3 fusion.59
  68.1 2.3 fusion.61
  70.4 2.2 fusion.63
  72.6 2.3 fusion.65
  75.0 2.4 fusion.67
  77.3 2.1 fusion.69
  79.5 2.3 fusion.71
  81.9 1.9 constant_dynamic-update-slice_fusion.1
  84.0 2.0 copy-done.2
  86.0 20.7 %fusion.10 = f32[128,27,512]{2,0,1:T(8,128)} fusion(bf16[128,27,4,8,128]{4,0,3,2,1:T(8,128)(2,1)} %fusion.71, bf16[512,4,8,128]{3,0,2,1:T(8,128)(2,1)S(1)} %constant_dynamic-update-slice_fusion), kind=kOutput, calls=%fused_computation.38 | convolution fusion | flops 14495514624 | bytes 39583744 | tf_op jit(solution)/shard_map/dot_general | solution.py:56
  106.7 8.0 %copy.18 = bf16[512,4,8,1,128]{0,2,4,1,3:T(8,128)(2,1)} copy(bf16[512,4,8,1,128]{4,0,2,1,3:T(8,128)(2,1)} %bitcast.144) | data formatting | bytes 8388608
  114.7 2.6 %pad.5.clone = bf16[512,4,8,1,136]{0,2,4,1,3:T(8,128)(2,1)S(1)} pad(bf16[512,4,8,1,128]{0,2,4,1,3:T(8,128)(2,1)} %copy.18, bf16[]{:T(256)} %constant.6.clone.1), padding=0_0x0_0x0_0x0_0x1_7 | pad | bytes 8650754 | tf_op jit(solution)/shard_map/broadcast_in_dim | solution.py:22
  117.3 1.7 copy.11
  119.2 16.9 %fusion.14 = f32[2,8,8,17,128]{4,2,3,1,0:T(8,128)S(1)} fusion(bf16[128,3,3,3,512]{4,0,3,2,1:T(8,128)(2,1)S(1)} %bitcast.142, bf16[512,4,8,1,7,2]{0,4,5,2,1,3:T(8,128)(2,1)S(1)} %slice.120, bf16[512,4,8,1,8,17]{0,4,5,2,1,3:T(8,128)(2,1)S(1)} %copy.11, pred[8,17]{0,1:T(8,128)(4,1)S(1)} %copy-done.4), kind=kOutput, calls=%fused_computation.40 | convolution fusion | flops 7074234368 | bytes 9568392 | tf_op jit(solution)/shard_map/conv_general_dilated | solution.py:21
  137.3 2.4 copy.14
  139.7 100.7 %all-reduce.3.cloned.1.call-done = f32[128,27,512]{2,0,1:T(8,128)} async-done(((f32[128,27,512]{2,0,1:T(8,128)}), f32[128,27,512]{2,0,1:T(8,128)}) %all-reduce.3.cloned.1.call-update) | async-done | bytes 7077904 | tf_op jit(solution)/shard_map/psum | solution.py:71
  240.4 7.3 %copy.48 = f32[128,27,512]{2,0,1:T(8,128)} copy(f32[128,27,512]{2,0,1:T(8,128)} %all-reduce.3.cloned.1.call-done) | data formatting | bytes 14155776
  (39 shorter events, 25.1 us)
Async XLA Ops:
  7.2 112.0 %copy-start = (bf16[128,27,512]{2,0,1:T(8,128)(2,1)S(1)}, bf16[128,27,512]{2,0,1:T(8,128)(2,1)}, u32[]{:S(2)}) copy-start(bf16[128,27,512]{2,0,1:T(8,128)(2,1)} %param.5) | copy-start | bytes 10616836
  7.2 51.7 %all-gather.2.cloned.1.call-start = ((), (), s32[]{:S(2)}) async-start(), calls=%async_computation | async-start | bytes 2621440 | tf_op jit(solution)/shard_map/all_gather | solution.py:67
  9.4 231.0 %all-reduce.3.cloned.1.call-start = ((), (), s32[]{:S(2)}) async-start(), calls=%async_computation.1 | async-start | bytes 14155776 | tf_op jit(solution)/shard_map/psum | solution.py:71
  10.6 22.5 %copy-start.1 = (bf16[128,2,8,128]{3,0,2,1:T(8,128)(2,1)}, bf16[128,2,8,128]{3,0,2,1:T(8,128)(2,1)S(1)}, u32[]{:S(2)}) copy-start(bf16[128,2,8,128]{3,0,2,1:T(8,128)(2,1)S(1)} %copy.13) | copy-start | bytes 1572868
  60.5 21.2 %collective-permute-start = (bf16[512,1,8,128]{3,0,2,1:T(8,128)(2,1)S(1)}, bf16[512,1,8,128]{3,0,2,1:T(8,128)(2,1)S(1)}, u32[]{:S(2)}, u32[]{:S(2)}) collective-permute-start(bf16[512,1,8,128]{3,0,2,1:T(8,128)(2,1)S(1)} %get-tuple-element.5), channel_id=1, source_target_pairs={{0,1},{1,2},{2,3},{4,5},{5,6},{6,7},{8,9},{9,10},{10,11},{12,13},{... | collective-permute-start | bytes 3145736 | tf_op jit(solution)/shard_map/ppermute | solution.py:12
  66.8 17.0 %collective-permute-start.1 = (bf16[512,1,8,128]{3,0,2,1:T(8,128)(2,1)S(1)}, bf16[512,1,8,128]{3,0,2,1:T(8,128)(2,1)S(1)}, u32[]{:S(2)}, u32[]{:S(2)}) collective-permute-start(bf16[512,1,8,128]{3,0,2,1:T(8,128)(2,1)S(1)} %get-tuple-element.4), channel_id=1, source_target_pairs={{1,0},{2,1},{3,2},{5,4},{6,5},{7,6},{9,8},{10,9},{11,10},{13,12},{... | collective-permute-start | bytes 3145736 | tf_op jit(solution)/shard_map/ppermute | solution.py:15
  83.9 2.0 copy-start.2
  106.6 12.6 %copy-start.4 = (pred[8,17]{0,1:T(8,128)(4,1)S(1)}, pred[8,17]{0,1:T(8,128)(4,1)}, u32[]{:S(2)}) copy-start(pred[8,17]{0,1:T(8,128)(4,1)} %constant.15) | copy-start | bytes 412
  119.2 17.1 %copy-start.3 = (f32[128]{0:T(128)S(1)}, f32[128]{0:T(128)}, u32[]{:S(2)}) copy-start(f32[128]{0:T(128)} %param.6) | copy-start | bytes 1540
Sparse Core Ops, SparseCore 0:
  10.2 48.6 all-gather.1
  106.8 133.5 all-reduce.2
where the time goes:
time: 255 us
  waiting for transfers between devices  125 us (49%)
  local copies, waits for them, and re-layouts  73.5 us (29%)
  matrix products  37.5 us (15%)
  between operations  14.2 us (6%)
  starting transfers between devices  3.13 us (1%)
    psum x1, waiting for transfers between devices, on_device(): weight_grad = lax.psum(partial_grads, 'space')  101 us
    unnamed x43, local copies, waits for them, and re-layouts  64.7 us
    all_gather x1, waiting for transfers between devices, on_device(): whole = lax.all_gather(volume, 'filt', axis=0, tiled=True)  24.5 us
    dot_general x1, matrix products, tap_grads(): lax.dot_general(slopes, flat, (((1,), (1,)), ((), ())), preferred_element...  20.7 us
    conv_general_dilated x1, matrix products, convolve(): lax.conv_general_dilated(slab[None], kernel, (1, 1, 1), [(0, 0), (1, 1),...  16.9 us
  transfers between devices with their start and end apart: 4, of which 2 were waited for; matrix products, arithmetic and copies ran while one was open for 31% of the time, Pallas kernels for 0%

commit v1 on v0

--- a/solution.py
+++ b/solution.py
@@ -28,47 +28,63 @@
     )[0]
 
 
-def shifted_slopes(upstream):
+def plane_shifts(upstream):
+    height = upstream.shape[2]
+    length = upstream.shape[3]
+    spread = jnp.pad(upstream, ((0, 0), (0, 0), (1, 1), (1, 1)))
+    copies = []
+    for tap in range(9):
+        second = tap // 3
+        third = tap % 3
+        copies.append(
+            spread[:, :, 2 - second : 2 - second + height, 2 - third : 2 - third + length]
+        )
+    stacked = jnp.stack(copies, 1)
+    return stacked.reshape(upstream.shape[0] * 9, -1)
+
+
+def tap_grads(rimmed, upstream):
     out_dev = upstream.shape[0]
     depth = upstream.shape[1]
-    height = upstream.shape[2]
-    length = upstream.shape[3]
-    spread = jnp.pad(upstream, ((0, 0), (2, 2), (1, 1), (1, 1)))
-    copies = []
-    for tap in range(27):
-        first = tap // 9
-        second = tap // 3 % 3
-        third = tap % 3
-        copies.append(
-            spread[
-                :,
-                2 - first : 4 - first + depth,
-                2 - second : 2 - second + height,
-                2 - third : 2 - third + length,
-            ]
+    shifted = plane_shifts(upstream)
+    rows = []
+    for first in range(3):
+        window = lax.slice_in_dim(rimmed, first, first + depth, axis=1)
+        flat = window.reshape(window.shape[0], -1)
+        product = lax.dot_general(
+            shifted, flat, (((1,), (1,)), ((), ())), preferred_element_type=jnp.float32
         )
-    stacked = jnp.stack(copies, 1)
-    return stacked.reshape(out_dev * 27, (depth + 2) * height * length)
+        rows.append(product.reshape(out_dev, 9, window.shape[0]))
+    return jnp.concatenate(rows, axis=1)
 
 
-def tap_grads(slab, slopes, out_dev):
-    flat = slab.reshape(slab.shape[0], -1)
-    product = lax.dot_general(
-        slopes, flat, (((1,), (1,)), ((), ())), preferred_element_type=jnp.float32
-    )
-    return product.reshape(out_dev, 27, slab.shape[0])
+def space_sum(grads):
+    count = lax.axis_size("space")
+    if count != 4 or grads.shape[2] % 2:
+        return lax.psum(grads, "space")
+    here = lax.axis_index("space")
+    core = here % 2
+    half = grads.shape[2] // 2
+    pair = [(i, i ^ 1) for i in range(count)]
+    across = [(i, i ^ 2) for i in range(count)]
+    mine = lax.dynamic_slice_in_dim(grads, core * half, half, axis=2)
+    other = lax.dynamic_slice_in_dim(grads, (1 - core) * half, half, axis=2)
+    mine = mine + lax.ppermute(other, "space", pair)
+    mine = mine + lax.ppermute(mine, "space", across)
+    theirs = lax.ppermute(mine, "space", pair)
+    low = jnp.where(core == 0, mine, theirs)
+    high = jnp.where(core == 0, theirs, mine)
+    return jnp.concatenate([low, high], axis=2)
 
 
 def on_device(volume, weight, bias, upstream):
     out_dev = weight.shape[0]
     in_all = weight.shape[2]
     kernel = weight.reshape(out_dev, 3, 3, 3, in_all).transpose(0, 4, 1, 2, 3)
-    slopes = shifted_slopes(upstream)
     whole = lax.all_gather(volume, "filt", axis=0, tiled=True)
     rimmed = padded(whole, (("space", 1),), 1)
+    weight_grad = space_sum(tap_grads(rimmed, upstream))
     pre = convolve(rimmed, kernel)
-    partial_grads = tap_grads(rimmed, slopes, out_dev)
-    weight_grad = lax.psum(partial_grads, "space")
     pre = pre + bias[:, None, None, None]
     features = jnp.where(pre > 0, pre, 0.3 * pre).astype(jnp.bfloat16)
     return (features, weight_grad)

time: 255 us -> 236 us (0.925)
  local copies, waits for them, and re-layouts: 73.5 us -> 38.7 us
  other arithmetic: 0.96 us -> 18.6 us
  starting transfers between devices: 3.13 us -> 10.6 us
  matrix products: 37.5 us -> 30.9 us
  waiting for transfers between devices: 125 us -> 122 us
    psum x1 -> x0, waiting for transfers between devices: 101 us -> none  [on_device(): weight_grad = lax.psum(partial_grads, 'space')]
    ppermute x0 -> x3, waiting for transfers between devices: none -> 84.5 us  [the longest x1 78.3 us: space_sum(): mine = mine + lax.ppermute(mine, 'space', across)]
    unnamed x43 -> x34, local copies, waits for them, and re-layouts: 64.7 us -> 29.1 us
    all_gather x1, waiting for transfers between devices: 24.5 us -> 37.5 us  [on_device(): whole = lax.all_gather(volume, 'filt', axis=0, tiled=True)]
    ppermute x0 -> x3, starting transfers between devices: none -> 7.52 us  [the longest x1 6.98 us: space_sum(): mine = mine + lax.ppermute(other, 'space', pair)]
    dot_general x1 -> x3, matrix products: 20.7 us -> 14 us  [tap_grads(): lax.dot_general(shifted, flat, (((1,), (1,)), ((), ())), preferred_elemen...]
    add x0 -> x2, other arithmetic: none -> 5.76 us  [the longest x1 3.54 us: space_sum(): mine = mine + lax.ppermute(other, 'space', pair)]
    concatenate x0 -> x2, other arithmetic: none -> 5.1 us  [the longest x1 3.89 us: space_sum(): return jnp.concatenate([low, high], axis=2)]
  transfers between devices with their start and end apart: 4 -> 6, of which waited for: 2 -> 3; matrix products, arithmetic and copies ran while one was open for 31% -> 25% of each run, Pallas kernels for 0% -> 0%
where the time goes in v1:
time: 236 us; the launch traced here: 235 us
  waiting for transfers between devices  122 us (52%)
  local copies, waits for them, and re-layouts  38.7 us (16%)
  matrix products  30.9 us (13%)
  other arithmetic  18.6 us (8%)
  between operations  14.3 us (6%)
  starting transfers between devices  10.6 us (4%)
    ppermute x1, waiting for transfers between devices, space_sum(): mine = mine + lax.ppermute(mine, 'space', across)  78.3 us
    all_gather x1, waiting for transfers between devices, on_device(): whole = lax.all_gather(volume, 'filt', axis=0, tiled=True)  37.5 us
    unnamed x34, local copies, waits for them, and re-layouts  29.1 us
    conv_general_dilated x1, matrix products, convolve(): lax.conv_general_dilated(slab[None], kernel, (1, 1, 1), [(0, 0), (1, 1),...  16.9 us
    dot_general x3, matrix products, tap_grads(): lax.dot_general(shifted, flat, (((1,), (1,)), ((), ())), preferred_elemen...  14 us
    ppermute x1, starting transfers between devices, space_sum(): mine = mine + lax.ppermute(other, 'space', pair)  6.98 us
    ppermute x1, waiting for transfers between devices, space_sum(): mine = mine + lax.ppermute(other, 'space', pair)  6.19 us
  transfers between devices with their start and end apart: 6, of which 3 were waited for; matrix products, arithmetic and copies ran while one was open for 25% of the time, Pallas kernels for 0%

profile of v1, /device:TPU:0, one launch (start us, length us, event | category | flops | bytes accessed | tf_op | source)
XLA Modules:
  0.0 235.2 jit_solution(11577630454897520898)
XLA Ops:
  7.2 2.1 copy.9
  9.4 2.0 copy.14
  11.4 2.1 fusion.34
  13.5 1.9 fusion.36
  15.3 2.0 fusion.38
  17.3 2.0 fusion.40
  21.3 37.5 %all-gather.2.cloned.1.call-done = bf16[512,2,8,128]{3,0,2,1:T(8,128)(2,1)} async-done(((bf16[128,2,8,128]{3,0,2,1:T(8,128)(2,1)}), bf16[512,2,8,128]{3,0,2,1:T(8,128)(2,1)}) %all-gather.2.cloned.1.call-update) | async-done | bytes 2097168 | tf_op jit(solution)/shard_map/all_gather | solution.py:84
  58.8 1.9 fusion.54
  66.6 4.6 %fusion.19 = f32[128,9,512]{2,0,1:T(8,128)S(1)} fusion(bf16[128,9,2,8,128]{4,0,3,2,1:T(8,128)(2,1)} %fusion.48, bf16[512,2,8,128]{3,0,2,1:T(8,128)(2,1)S(1)} %copy-done.5), kind=kOutput, calls=%fused_computation.34 | convolution fusion | flops 2415919104 | bytes 9175040 | tf_op jit(solution)/shard_map/dot_general | solution.py:54
  71.2 4.9 %fusion.22 = f32[128,9,512]{2,0,1:T(8,128)S(1)} fusion(bf16[128,9,2,8,128]{4,0,3,2,1:T(8,128)(2,1)} %fusion.48, bf16[512,2,8,128]{3,0,2,1:T(8,128)(2,1)S(1)} %copy-done.5, bf16[512,1,8,128]{3,0,2,1:T(8,128)(2,1)S(1)} %collective-permute-done), kind=kOutput, calls=%fused_computation.35 | convolution fusion | flops 2416967680 | bytes 10223616 | tf_op jit(solution)/shard_map/dot_general | solution.py:54
  77.2 4.5 %fusion.25 = f32[128,9,512]{2,0,1:T(8,128)S(1)} fusion(bf16[128,9,2,8,128]{4,0,3,2,1:T(8,128)(2,1)} %fusion.48, bf16[512,1,8,128]{3,0,2,1:T(8,128)(2,1)S(1)} %collective-permute-done.1, bf16[512,2,8,128]{3,0,2,1:T(8,128)(2,1)S(1)} %copy-done.5), kind=kOutput, calls=%fused_computation.36 | convolution fusion | flops 2416967680 | bytes 10223616 | tf_op jit(solution)/shard_map/dot_general | solution.py:54
  82.9 3.0 %copy-done.4 = f32[128,27,512]{2,0,1:T(8,128)} copy-done((f32[128,27,512]{2,0,1:T(8,128)}, f32[128,27,512]{2,0,1:T(8,128)S(1)}, u32[]{:S(2)}) %copy-start.4) | copy-done | bytes 7077912
  85.9 2.2 constant_dynamic-slice_fusion
  88.1 7.0 %collective-permute-start.2 = (f32[128,27,256]{2,0,1:T(8,128)}, f32[128,27,256]{2,0,1:T(8,128)}, u32[]{:S(2)}, u32[]{:S(2)}) collective-permute-start(f32[128,27,256]{2,0,1:T(8,128)} %constant_dynamic-slice_fusion), channel_id=1, source_target_pairs={{0,1},{1,0},{2,3},{3,2},{4,5},{5,4},{6,7},{7,6},{8,9},{9,8},{10,11... | collective-permute-start | bytes 10616840 | tf_op jit(solution)/shard_map/ppermute | solution.py:72
  95.1 6.2 %collective-permute-done.2 = f32[128,27,256]{2,0,1:T(8,128)} collective-permute-done((f32[128,27,256]{2,0,1:T(8,128)}, f32[128,27,256]{2,0,1:T(8,128)}, u32[]{:S(2)}, u32[]{:S(2)}) %collective-permute-start.2) | collective-permute-done | bytes 3538976 | tf_op jit(solution)/shard_map/ppermute | solution.py:72
  101.3 3.5 %dynamic-slice_add_fusion = f32[128,27,256]{2,0,1:T(8,128)S(1)} fusion(f32[128,27,256]{2,0,1:T(8,128)} %collective-permute-done.2, f32[128,27,512]{2,0,1:T(8,128)} %copy-done.4, s32[]{:T(128)S(6)} %select_n.32), kind=kLoop, calls=%fused_computation.11 | loop fusion | flops 884736 | bytes 10616836 | tf_op jit(solution)/shard_map/add | solution.py:72
  105.4 78.3 %collective-permute-done.3 = f32[128,27,256]{2,0,1:T(8,128)S(1)} collective-permute-done((f32[128,27,256]{2,0,1:T(8,128)S(1)}, f32[128,27,256]{2,0,1:T(8,128)S(1)}, u32[]{:S(2)}, u32[]{:S(2)}) %collective-permute-start.3) | collective-permute-done | bytes 3538976 | tf_op jit(solution)/shard_map/ppermute | solution.py:73
  183.7 2.2 add.32
  185.9 3.8 %maximum_bitcast_fusion = bf16[512,4,8,1,128]{4,0,2,1,3:T(8,128)(2,1)} fusion(bf16[512,1,8,128]{3,0,2,1:T(8,128)(2,1)} %copy-done.8, bf16[512,2,8,128]{3,0,2,1:T(8,128)(2,1)} %all-gather.2.cloned.1.call-done, bf16[512,1,8,128]{3,0,2,1:T(8,128)(2,1)} %copy-done.7), kind=kLoop, calls=%fused_computation.10 | loop fusion | flops 4194304 | bytes 8388608 | tf_op jit(solution)/shard_map/broadcast_in_dim | solution.py:22
  189.7 7.9 %copy.24 = bf16[512,4,8,1,128]{0,2,4,1,3:T(8,128)(2,1)} copy(bf16[512,4,8,1,128]{4,0,2,1,3:T(8,128)(2,1)} %maximum_bitcast_fusion) | data formatting | bytes 8388608
  197.6 2.5 %pad.5.clone = bf16[512,4,8,1,136]{0,2,4,1,3:T(8,128)(2,1)S(1)} pad(bf16[512,4,8,1,128]{0,2,4,1,3:T(8,128)(2,1)} %copy.24, bf16[]{:T(256)} %constant.26.clone.1), padding=0_0x0_0x0_0x0_0x1_7 | pad | bytes 8650754 | tf_op jit(solution)/shard_map/broadcast_in_dim | solution.py:22
  202.0 16.9 %fusion.28 = f32[2,8,8,17,128]{4,2,3,1,0:T(8,128)S(1)} fusion(bf16[128,3,3,3,512]{4,0,3,2,1:T(8,128)(2,1)S(1)} %bitcast.101, bf16[512,4,8,1,7,2]{0,4,5,2,1,3:T(8,128)(2,1)S(1)} %slice.55, bf16[512,4,8,1,8,17]{0,4,5,2,1,3:T(8,128)(2,1)S(1)} %copy.12, pred[8,17]{0,1:T(8,128)(4,1)S(1)} %copy-done.10), kind=kOutput, calls=%fused_computation.37 | convolution fusion | flops 7074234368 | bytes 9568392 | tf_op jit(solution)/shard_map/conv_general_dilated | solution.py:21
  220.6 3.8 %broadcast_select_fusion.1 = (f32[128,27,256]{2,0,1:T(8,128)S(1)}, f32[128,27,256]{2,0,1:T(8,128)S(1)}) fusion(f32[128,27,256]{2,0,1:T(8,128)} %add.32, f32[128,27,256]{2,0,1:T(8,128)} %collective-permute-done.4, pred[]{:T(512)S(6)} %eq.6), kind=kLoop, calls=%fused_computation.33 | loop fusion | flops 1769472 | bytes 14155777 | tf_op jit(solution)/shard_map/jit(_where)/select_n | solution.py:75
  224.4 3.9 %pad_maximum_fusion.1 = f32[128,27,512]{2,0,1:T(8,128)} fusion(f32[128,27,256]{2,0,1:T(8,128)S(1)} %get-tuple-element.5, f32[128,27,256]{2,0,1:T(8,128)S(1)} %get-tuple-element.4), kind=kLoop, calls=%fused_computation.3 | loop fusion | flops 1769472 | bytes 14155776 | tf_op jit(solution)/shard_map/concatenate | solution.py:77
  (41 shorter events, 14.2 us)
Async XLA Ops:
  7.2 194.8 %copy-start = (bf16[128,27,512]{2,0,1:T(8,128)(2,1)S(1)}, bf16[128,27,512]{2,0,1:T(8,128)(2,1)}, u32[]{:S(2)}) copy-start(bf16[128,27,512]{2,0,1:T(8,128)(2,1)} %param.5) | copy-start | bytes 10616836
  7.2 51.7 %all-gather.2.cloned.1.call-start = ((), (), s32[]{:S(2)}) async-start(), calls=%async_computation | async-start | bytes 2621440 | tf_op jit(solution)/shard_map/all_gather | solution.py:84
  11.4 8.0 %copy-start.6 = (bf16[128,2,8,128]{3,2,1,0:T(8,128)(2,1)S(1)}, bf16[128,2,8,128]{3,2,1,0:T(8,128)(2,1)}, u32[]{:S(2)}) copy-start(bf16[128,2,8,128]{3,2,1,0:T(8,128)(2,1)} %param.7) | copy-start | bytes 1572868
  11.4 8.9 %copy-start.2 = (bf16[128,2,8,128]{3,0,2,1:T(8,128)(2,1)S(1)}, bf16[128,2,8,128]{3,0,2,1:T(8,128)(2,1)}, u32[]{:S(2)}) copy-start(bf16[128,2,8,128]{3,0,2,1:T(8,128)(2,1)} %copy.14) | copy-start | bytes 1572868
  58.8 3.7 %copy-start.3 = (bf16[128,2,8,128]{3,0,2,1:T(8,128)(2,1)S(1)}, bf16[128,2,8,128]{3,0,2,1:T(8,128)(2,1)}, u32[]{:S(2)}) copy-start(bf16[128,2,8,128]{3,0,2,1:T(8,128)(2,1)} %copy.14) | copy-start | bytes 1572868
  58.8 7.8 %copy-start.5 = (bf16[512,2,8,128]{3,0,2,1:T(8,128)(2,1)S(1)}, bf16[512,2,8,128]{3,0,2,1:T(8,128)(2,1)}, u32[]{:S(2)}) copy-start(bf16[512,2,8,128]{3,0,2,1:T(8,128)(2,1)} %all-gather.2.cloned.1.call-done) | copy-start | bytes 6291460
  60.7 10.5 %collective-permute-start = (bf16[512,1,8,128]{3,0,2,1:T(8,128)(2,1)S(1)}, bf16[512,1,8,128]{3,0,2,1:T(8,128)(2,1)S(1)}, u32[]{:S(2)}, u32[]{:S(2)}) collective-permute-start(bf16[512,1,8,128]{3,0,2,1:T(8,128)(2,1)S(1)} %get-tuple-element.6), channel_id=1, source_target_pairs={{0,1},{1,2},{2,3},{4,5},{5,6},{6,7},{8,9},{9,10},{10,11},{12,13},{... | collective-permute-start | bytes 3145736 | tf_op jit(solution)/shard_map/ppermute | solution.py:12
  65.3 10.8 %collective-permute-start.1 = (bf16[512,1,8,128]{3,0,2,1:T(8,128)(2,1)S(1)}, bf16[512,1,8,128]{3,0,2,1:T(8,128)(2,1)S(1)}, u32[]{:S(2)}, u32[]{:S(2)}) collective-permute-start(bf16[512,1,8,128]{3,0,2,1:T(8,128)(2,1)S(1)} %get-tuple-element.7), channel_id=1, source_target_pairs={{1,0},{2,1},{3,2},{5,4},{6,5},{7,6},{9,8},{10,9},{11,10},{13,12},{... | collective-permute-start | bytes 3145736 | tf_op jit(solution)/shard_map/ppermute | solution.py:15
  71.2 5.0 %copy-start.7 = (bf16[512,1,8,128]{3,0,2,1:T(8,128)(2,1)}, bf16[512,1,8,128]{3,0,2,1:T(8,128)(2,1)S(1)}, u32[]{:S(2)}) copy-start(bf16[512,1,8,128]{3,0,2,1:T(8,128)(2,1)S(1)} %collective-permute-done) | copy-start | bytes 3145732
  76.2 1.0 copy-start.8
  82.9 3.0 %copy-start.4 = (f32[128,27,512]{2,0,1:T(8,128)}, f32[128,27,512]{2,0,1:T(8,128)S(1)}, u32[]{:S(2)}) copy-start(f32[128,27,512]{2,0,1:T(8,128)S(1)} %pad_maximum_fusion) | copy-start | bytes 21233668
  88.1 13.2 %collective-permute-start.2 = (f32[128,27,256]{2,0,1:T(8,128)}, f32[128,27,256]{2,0,1:T(8,128)}, u32[]{:S(2)}, u32[]{:S(2)}) collective-permute-start(f32[128,27,256]{2,0,1:T(8,128)} %constant_dynamic-slice_fusion), channel_id=1, source_target_pairs={{0,1},{1,0},{2,3},{3,2},{4,5},{5,4},{6,7},{7,6},{8,9},{9,8},{10,11... | collective-permute-start | bytes 10616840 | tf_op jit(solution)/shard_map/ppermute | solution.py:72
  104.8 78.9 %collective-permute-start.3 = (f32[128,27,256]{2,0,1:T(8,128)S(1)}, f32[128,27,256]{2,0,1:T(8,128)S(1)}, u32[]{:S(2)}, u32[]{:S(2)}) collective-permute-start(f32[128,27,256]{2,0,1:T(8,128)S(1)} %dynamic-slice_add_fusion), channel_id=1, source_target_pairs={{0,2},{1,3},{2,0},{3,1},{4,6},{5,7},{6,4},{7,5},{8,10},{9,11},{10,... | collective-permute-start | bytes 10616840 | tf_op jit(solution)/shard_map/ppermute | solution.py:73
  185.9 34.7 %collective-permute-start.4 = (f32[128,27,256]{2,0,1:T(8,128)}, f32[128,27,256]{2,0,1:T(8,128)}, u32[]{:S(2)}, u32[]{:S(2)}) collective-permute-start(f32[128,27,256]{2,0,1:T(8,128)} %add.32), channel_id=1, source_target_pairs={{0,1},{1,0},{2,3},{3,2},{4,5},{5,4},{6,7},{7,6},{8,9},{9,8},{10,11... | collective-permute-start | bytes 10616840 | tf_op jit(solution)/shard_map/ppermute | solution.py:74
  200.1 1.9 copy-start.10
  202.0 17.1 %copy-start.9 = (f32[128]{0:T(128)S(1)}, f32[128]{0:T(128)}, u32[]{:S(2)}) copy-start(f32[128]{0:T(128)} %param.6) | copy-start | bytes 1540
  224.4 3.9 %copy-start.1 = (bf16[128,27,512]{2,0,1:T(8,128)(2,1)S(1)}, bf16[128,27,512]{2,0,1:T(8,128)(2,1)}, u32[]{:S(2)}) copy-start(bf16[128,27,512]{2,0,1:T(8,128)(2,1)} %param.5) | copy-start | bytes 10616836
Sparse Core Ops, SparseCore 0:
  10.2 48.6 all-gather.1

commit v2 on v1

--- a/solution.py
+++ b/solution.py
@@ -43,10 +43,7 @@
     return stacked.reshape(upstream.shape[0] * 9, -1)
 
 
-def tap_grads(rimmed, upstream):
-    out_dev = upstream.shape[0]
-    depth = upstream.shape[1]
-    shifted = plane_shifts(upstream)
+def tap_grads(rimmed, shifted, out_dev, depth):
     rows = []
     for first in range(3):
         window = lax.slice_in_dim(rimmed, first, first + depth, axis=1)
@@ -58,35 +55,57 @@
     return jnp.concatenate(rows, axis=1)
 
 
-def space_sum(grads):
+def space_sum(grads, beside=None, operand=None):
     count = lax.axis_size("space")
-    if count != 4 or grads.shape[2] % 2:
-        return lax.psum(grads, "space")
-    here = lax.axis_index("space")
-    core = here % 2
-    half = grads.shape[2] // 2
+    if count != 4 or grads.shape[0] % 2:
+        if beside is None:
+            return lax.psum(grads, "space")
+        return lax.psum(grads, "space"), beside(operand)
+    core = lax.axis_index("space") % 2
+    half = grads.shape[0] // 2
     pair = [(i, i ^ 1) for i in range(count)]
     across = [(i, i ^ 2) for i in range(count)]
-    mine = lax.dynamic_slice_in_dim(grads, core * half, half, axis=2)
-    other = lax.dynamic_slice_in_dim(grads, (1 - core) * half, half, axis=2)
+    mine = lax.dynamic_slice_in_dim(grads, core * half, half, axis=0)
+    other = lax.dynamic_slice_in_dim(grads, (1 - core) * half, half, axis=0)
     mine = mine + lax.ppermute(other, "space", pair)
-    mine = mine + lax.ppermute(mine, "space", across)
+    if beside is not None:
+        mine, operand = lax.optimization_barrier((mine, operand))
+    arrived = lax.ppermute(mine, "space", across)
+    if beside is not None:
+        result = beside(operand)
+        arrived, result = lax.optimization_barrier((arrived, result))
+    mine = mine + arrived
     theirs = lax.ppermute(mine, "space", pair)
     low = jnp.where(core == 0, mine, theirs)
     high = jnp.where(core == 0, theirs, mine)
-    return jnp.concatenate([low, high], axis=2)
+    summed = jnp.concatenate([low, high], axis=0)
+    if beside is None:
+        return summed
+    return summed, result
 
 
 def on_device(volume, weight, bias, upstream):
     out_dev = weight.shape[0]
     in_all = weight.shape[2]
+    in_dev = volume.shape[0]
+    depth = upstream.shape[1]
     kernel = weight.reshape(out_dev, 3, 3, 3, in_all).transpose(0, 4, 1, 2, 3)
+    shifted = plane_shifts(upstream)
+    own = padded(volume, (("space", 1),), 1)
+    own_grads = space_sum(tap_grads(own, shifted, out_dev, depth))
     whole = lax.all_gather(volume, "filt", axis=0, tiled=True)
+    whole, own_grads = lax.optimization_barrier((whole, own_grads))
     rimmed = padded(whole, (("space", 1),), 1)
-    weight_grad = space_sum(tap_grads(rimmed, upstream))
-    pre = convolve(rimmed, kernel)
-    pre = pre + bias[:, None, None, None]
-    features = jnp.where(pre > 0, pre, 0.3 * pre).astype(jnp.bfloat16)
+    start = lax.axis_index("filt") * in_dev
+    rolled = jnp.roll(rimmed, -start, axis=0)
+    rest = lax.slice_in_dim(rolled, in_dev, in_all, axis=0)
+
+    def forward(slab):
+        pre = convolve(slab, kernel) + bias[:, None, None, None]
+        return jnp.where(pre > 0, pre, 0.3 * pre).astype(jnp.bfloat16)
+
+    rest_grads, features = space_sum(tap_grads(rest, shifted, out_dev, depth), forward, rimmed)
+    weight_grad = jnp.roll(jnp.concatenate([own_grads, rest_grads], axis=2), start, axis=2)
     return (features, weight_grad)
 
 

time: 236 us -> 220 us (0.932)
  waiting for transfers between devices: 122 us -> 78 us
  starting transfers between devices: 10.6 us -> 26.7 us
  matrix products: 30.9 us -> 41.8 us
    ppermute x1 -> x2, waiting for transfers between devices: 78.3 us -> 49 us  [space_sum(): arrived = lax.ppermute(mine, 'space', across)]
    all_gather x1, waiting for transfers between devices: 37.5 us -> 15 us  [on_device(): whole = lax.all_gather(volume, 'filt', axis=0, tiled=True)]
    dot_general x3 -> x6, matrix products: 14 us -> 25 us  [tap_grads(): lax.dot_general(shifted, flat, (((1,), (1,)), ((), ())), preferred_elemen...]
    ppermute x1 -> x2, starting transfers between devices: 6.98 us -> 14.7 us  [space_sum(): mine = mine + lax.ppermute(other, 'space', pair)]
    ppermute x1 -> x2, waiting for transfers between devices: 0.01 us -> 6.48 us  [space_sum(): theirs = lax.ppermute(mine, 'space', pair)]
    unnamed x34 -> x32, local copies, waits for them, and re-layouts: 29.1 us -> 24.6 us
    concatenate x1 -> x3, other arithmetic: 3.89 us -> 8.12 us  [the longest x1 4.56 us: on_device(): jnp.roll(jnp.concatenate([own_grads, rest_grads], axis=2), start, axis=2)]
    ppermute x1 -> x2, starting transfers between devices: 1.77 us -> 5.75 us  [padded(): lax.ppermute(lax.slice_in_dim(block, block.shape[dim] - width, None, axis...]
  transfers between devices with their start and end apart: 6 -> 11, of which waited for: 3 -> 9; matrix products, arithmetic and copies ran while one was open for 25% -> 26% of each run, Pallas kernels for 0% -> 0%
where the time goes in v2:
time: 220 us; the launch traced here: 219 us
  waiting for transfers between devices  78 us (35%)
  matrix products  41.8 us (19%)
  local copies, waits for them, and re-layouts  37.7 us (17%)
  starting transfers between devices  26.7 us (12%)
  other arithmetic  20.2 us (9%)
  between operations  14.4 us (7%)
    ppermute x2, waiting for transfers between devices, space_sum(): arrived = lax.ppermute(mine, 'space', across)  49 us
    dot_general x6, matrix products, tap_grads(): lax.dot_general(shifted, flat, (((1,), (1,)), ((), ())), preferred_elemen...  25 us
    unnamed x32, local copies, waits for them, and re-layouts  24.6 us
    conv_general_dilated x1, matrix products, convolve(): lax.conv_general_dilated(slab[None], kernel, (1, 1, 1), [(0, 0), (1, 1),...  16.9 us
    all_gather x1, waiting for transfers between devices, on_device(): whole = lax.all_gather(volume, 'filt', axis=0, tiled=True)  15 us
    ppermute x2, starting transfers between devices, space_sum(): mine = mine + lax.ppermute(other, 'space', pair)  14.7 us
    ppermute x2, waiting for transfers between devices, space_sum(): mine = mine + lax.ppermute(other, 'space', pair)  6.95 us
    ppermute x2, waiting for transfers between devices, space_sum(): theirs = lax.ppermute(mine, 'space', pair)  6.48 us
  transfers between devices with their start and end apart: 11, of which 9 were waited for; matrix products, arithmetic and copies ran while one was open for 26% of the time, Pallas kernels for 0%

profile of v2, /device:TPU:0, one launch (start us, length us, event | category | flops | bytes accessed | tf_op | source)
XLA Modules:
  0.0 219.0 jit_solution(10306287583684926686)
XLA Ops:
  11.2 3.1 %collective-permute-start = (bf16[128,1,8,128]{3,0,2,1:T(8,128)(2,1)}, bf16[128,1,8,128]{3,0,2,1:T(8,128)(2,1)}, u32[]{:S(2)}, u32[]{:S(2)}) collective-permute-start(bf16[128,1,8,128]{3,0,2,1:T(8,128)(2,1)} %get-tuple-element.22), channel_id=1, source_target_pairs={{0,1},{1,2},{2,3},{4,5},{5,6},{6,7},{8,9},{9,10},{10,11},{12,13},{... | collective-permute-start | bytes 786440 | tf_op jit(solution)/shard_map/ppermute | solution.py:12
  25.4 3.9 %convolution_bitcast_fusion.1 = f32[128,9,128]{2,0,1:T(8,128)S(1)} fusion(bf16[128,9,2,8,128]{4,0,3,2,1:T(8,128)(2,1)} %fusion.41, bf16[128,2,8,128,1]{3,2,1,0,4:T(8,128)(2,1)} %bitcast.143), kind=kOutput, calls=%fused_computation.49 | convolution fusion | flops 603979776 | bytes 5832704 | tf_op jit(solution)/shard_map/dot_general | solution.py:51
  29.4 3.8 %convolution_bitcast_fusion = f32[128,9,128]{2,0,1:T(8,128)S(1)} fusion(bf16[128,9,2,8,128]{4,0,3,2,1:T(8,128)(2,1)} %fusion.41, bf16[128,1,8,128]{3,0,2,1:T(8,128)(2,1)} %collective-permute-done.1, bf16[128,2,8,128]{3,0,2,1:T(8,128)(2,1)S(1)} %copy-done.5), kind=kOutput, calls=%fused_computation.48 | convolution fusion | flops 604241920 | bytes 6094848 | tf_op jit(solution)/shard_map/dot_general | solution.py:51
  33.2 3.8 %convolution_bitcast_fusion.2 = f32[128,9,128]{2,0,1:T(8,128)S(1)} fusion(bf16[128,9,2,8,128]{4,0,3,2,1:T(8,128)(2,1)} %fusion.41, bf16[128,2,8,128]{3,0,2,1:T(8,128)(2,1)S(1)} %copy-done.5, bf16[128,1,8,128]{3,0,2,1:T(8,128)(2,1)} %collective-permute-done), kind=kOutput, calls=%fused_computation.50 | convolution fusion | flops 604241920 | bytes 6094848 | tf_op jit(solution)/shard_map/dot_general | solution.py:51
  39.3 2.5 %collective-permute-start.2 = (f32[64,27,128]{2,0,1:T(8,128)}, f32[64,27,128]{2,0,1:T(8,128)}, u32[]{:S(2)}, u32[]{:S(2)}) collective-permute-start(f32[64,27,128]{2,0,1:T(8,128)} %constant_dynamic-slice_fusion.1), channel_id=1, source_target_pairs={{0,1},{1,0},{2,3},{3,2},{4,5},{5,4},{6,7},{7,6},{8,9},{9,8},{10,11... | collective-permute-start | bytes 2654216 | tf_op jit(solution)/shard_map/ppermute | solution.py:70
  41.9 2.4 %collective-permute-done.2 = f32[64,27,128]{2,0,1:T(8,128)} collective-permute-done((f32[64,27,128]{2,0,1:T(8,128)}, f32[64,27,128]{2,0,1:T(8,128)}, u32[]{:S(2)}, u32[]{:S(2)}) %collective-permute-start.2) | collective-permute-done | bytes 884768 | tf_op jit(solution)/shard_map/ppermute | solution.py:70
  47.9 19.9 %collective-permute-done.3 = f32[64,27,128]{2,0,1:T(8,128)S(1)} collective-permute-done((f32[64,27,128]{2,0,1:T(8,128)S(1)}, f32[64,27,128]{2,0,1:T(8,128)S(1)}, u32[]{:S(2)}, u32[]{:S(2)}) %collective-permute-start.3) | collective-permute-done | bytes 884768 | tf_op jit(solution)/shard_map/ppermute | solution.py:73
  68.9 2.8 %collective-permute-done.4 = f32[64,27,128]{2,0,1:T(8,128)} collective-permute-done((f32[64,27,128]{2,0,1:T(8,128)}, f32[64,27,128]{2,0,1:T(8,128)}, u32[]{:S(2)}, u32[]{:S(2)}) %collective-permute-start.4) | collective-permute-done | bytes 884768 | tf_op jit(solution)/shard_map/ppermute | solution.py:78
  74.5 15.0 %all-gather.2.cloned.1.call-done = bf16[512,2,8,128]{3,0,2,1:T(8,128)(2,1)} async-done(((bf16[128,2,8,128]{3,0,2,1:T(8,128)(2,1)}), bf16[512,2,8,128]{3,0,2,1:T(8,128)(2,1)}) %all-gather.2.cloned.1.call-update) | async-done | bytes 2097168 | tf_op jit(solution)/shard_map/all_gather | solution.py:96
  89.5 3.1 %fusion.55 = (bf16[512,1,8,128]{3,0,2,1:T(8,128)(2,1)}, bf16[512,1,8,128]{3,0,2,1:T(8,128)(2,1)}) fusion(bf16[512,2,8,128]{3,0,2,1:T(8,128)(2,1)} %all-gather.2.cloned.1.call-done), kind=kLoop, calls=%fused_computation.92 | loop fusion | bytes 4194304 | tf_op jit(solution)/shard_map/slice | solution.py:15
  92.6 2.7 %collective-permute-start.5 = (bf16[512,1,8,128]{3,0,2,1:T(8,128)(2,1)}, bf16[512,1,8,128]{3,0,2,1:T(8,128)(2,1)}, u32[]{:S(2)}, u32[]{:S(2)}) collective-permute-start(bf16[512,1,8,128]{3,0,2,1:T(8,128)(2,1)} %get-tuple-element.19), channel_id=1, source_target_pairs={{0,1},{1,2},{2,3},{4,5},{5,6},{6,7},{8,9},{9,10},{10,11},{12,13},{... | collective-permute-start | bytes 3145736 | tf_op jit(solution)/shard_map/ppermute | solution.py:12
  101.9 2.2 %fusion.13 = bf16[512,4,8,128]{3,0,2,1:T(8,128)(2,1)S(1)} fusion(s32[]{:T(128)S(6)} %select_n.74, bf16[512,4,8,128]{3,0,2,1:T(8,128)(2,1)S(1)} %constant_dynamic-update-slice_fusion), kind=kLoop, calls=%fused_computation.22 | loop fusion | flops 8388608 | bytes 8388612 | tf_op jit(solution)/shard_map/jit(_roll_dynamic)/concatenate | solution.py:100
  104.1 4.5 %fusion.19 = f32[128,9,384]{2,0,1:T(8,128)S(1)} fusion(bf16[128,9,2,8,128]{4,0,3,2,1:T(8,128)(2,1)} %fusion.41, bf16[512,4,8,128]{3,0,2,1:T(8,128)(2,1)S(1)} %fusion.13), kind=kOutput, calls=%fused_computation.43 | convolution fusion | flops 1811939328 | bytes 8060928 | tf_op jit(solution)/shard_map/dot_general | solution.py:51
  108.7 4.5 %fusion.18 = f32[128,9,384]{2,0,1:T(8,128)S(1)} fusion(bf16[128,9,2,8,128]{4,0,3,2,1:T(8,128)(2,1)} %fusion.41, bf16[512,4,8,128]{3,0,2,1:T(8,128)(2,1)S(1)} %fusion.13), kind=kOutput, calls=%fused_computation.42 | convolution fusion | flops 1811939328 | bytes 8060928 | tf_op jit(solution)/shard_map/dot_general | solution.py:51
  113.2 4.5 %fusion.20 = f32[128,9,384]{2,0,1:T(8,128)S(1)} fusion(bf16[128,9,2,8,128]{4,0,3,2,1:T(8,128)(2,1)} %fusion.41, bf16[512,4,8,128]{3,0,2,1:T(8,128)(2,1)S(1)} %fusion.13), kind=kOutput, calls=%fused_computation.44 | convolution fusion | flops 1811939328 | bytes 8060928 | tf_op jit(solution)/shard_map/dot_general | solution.py:51
  118.5 12.1 %collective-permute-start.7 = (f32[64,27,384]{2,0,1:T(8,128)S(1)}, f32[64,27,384]{2,0,1:T(8,128)S(1)}, u32[]{:S(2)}, u32[]{:S(2)}) collective-permute-start(f32[64,27,384]{2,0,1:T(8,128)S(1)} %constant_dynamic-slice_fusion), channel_id=1, source_target_pairs={{0,1},{1,0},{2,3},{3,2},{4,5},{5,4},{6,7},{7,6},{8,9},{9,8},{10,11... | collective-permute-start | bytes 7962632 | tf_op jit(solution)/shard_map/ppermute | solution.py:70
  130.6 4.6 %collective-permute-done.7 = f32[64,27,384]{2,0,1:T(8,128)S(1)} collective-permute-done((f32[64,27,384]{2,0,1:T(8,128)S(1)}, f32[64,27,384]{2,0,1:T(8,128)S(1)}, u32[]{:S(2)}, u32[]{:S(2)}) %collective-permute-start.7) | collective-permute-done | bytes 2654240 | tf_op jit(solution)/shard_map/ppermute | solution.py:70
  138.7 7.8 %copy.44 = bf16[512,4,8,1,128]{0,2,4,1,3:T(8,128)(2,1)} copy(bf16[512,4,8,1,128]{4,0,2,1,3:T(8,128)(2,1)} %bitcast.140) | data formatting | bytes 8388608
  146.5 2.5 %pad.5.clone = bf16[512,4,8,1,136]{0,2,4,1,3:T(8,128)(2,1)S(1)} pad(bf16[512,4,8,1,128]{0,2,4,1,3:T(8,128)(2,1)} %copy.44, bf16[]{:T(256)} %constant.55.clone.1), padding=0_0x0_0x0_0x0_0x1_7 | pad | bytes 8650754 | tf_op jit(solution)/shard_map/broadcast_in_dim | solution.py:22
  150.9 16.9 %fusion.21 = f32[2,8,8,17,128]{4,2,3,1,0:T(8,128)S(1)} fusion(bf16[128,3,3,3,512]{4,0,3,2,1:T(8,128)(2,1)S(1)} %bitcast.139, bf16[512,4,8,1,7,2]{0,4,5,2,1,3:T(8,128)(2,1)S(1)} %slice.82, bf16[512,4,8,1,8,17]{0,4,5,2,1,3:T(8,128)(2,1)S(1)} %copy.26, pred[8,17]{0,1:T(8,128)(4,1)S(1)} %copy-done.8), kind=kOutput, calls=%fused_computation.47 | convolution fusion | flops 7074234368 | bytes 9568392 | tf_op jit(solution)/shard_map/conv_general_dilated | solution.py:21
  168.3 29.0 %collective-permute-done.8 = f32[64,27,384]{2,0,1:T(8,128)} collective-permute-done((f32[64,27,384]{2,0,1:T(8,128)}, f32[64,27,384]{2,0,1:T(8,128)}, u32[]{:S(2)}, u32[]{:S(2)}) %collective-permute-start.8) | collective-permute-done | bytes 2654240 | tf_op jit(solution)/shard_map/ppermute | solution.py:73
  197.3 3.0 %add.64 = f32[64,27,384]{2,0,1:T(8,128)S(1)} add(f32[64,27,384]{2,0,1:T(8,128)} %dynamic-slice_add_fusion, f32[64,27,384]{2,0,1:T(8,128)} %collective-permute-done.8) | non-fusion elementwise | flops 663552 | bytes 7962624 | tf_op jit(solution)/shard_map/add | solution.py:77
  201.7 3.7 %collective-permute-done.9 = f32[64,27,384]{2,0,1:T(8,128)} collective-permute-done((f32[64,27,384]{2,0,1:T(8,128)S(1)}, f32[64,27,384]{2,0,1:T(8,128)}, u32[]{:S(2)}, u32[]{:S(2)}) %collective-permute-start.9) | collective-permute-done | bytes 2654240 | tf_op jit(solution)/shard_map/ppermute | solution.py:78
  207.6 4.6 %fusion.3 = f32[128,27,512]{2,0,1:T(8,128)} fusion(s32[]{:T(128)S(6)} %select_n.80, f32[128,27,128]{2,0,1:T(8,128)S(1)} %copy-done.4, f32[64,27,384]{2,0,1:T(8,128)S(1)} %get-tuple-element.17, f32[64,27,384]{2,0,1:T(8,128)S(1)} %get-tuple-element.16), kind=kLoop, calls=%fused_computation.12 | loop fusion | flops 8847360 | bytes 14155780 | tf_op jit(solution)/shard_map/jit(_roll_dynamic)/concatenate | solution.py:108
  (60 shorter events, 41.7 us)
Async XLA Ops:
  7.2 143.7 %copy-start = (bf16[128,27,512]{2,0,1:T(8,128)(2,1)S(1)}, bf16[128,27,512]{2,0,1:T(8,128)(2,1)}, u32[]{:S(2)}) copy-start(bf16[128,27,512]{2,0,1:T(8,128)(2,1)} %param.5) | copy-start | bytes 10616836
  7.2 82.3 %all-gather.2.cloned.1.call-start = ((), (), s32[]{:S(2)}) async-start(), calls=%async_computation | async-start | bytes 2621440 | tf_op jit(solution)/shard_map/all_gather | solution.py:96
  11.2 21.9 %collective-permute-start = (bf16[128,1,8,128]{3,0,2,1:T(8,128)(2,1)}, bf16[128,1,8,128]{3,0,2,1:T(8,128)(2,1)}, u32[]{:S(2)}, u32[]{:S(2)}) collective-permute-start(bf16[128,1,8,128]{3,0,2,1:T(8,128)(2,1)} %get-tuple-element.22), channel_id=1, source_target_pairs={{0,1},{1,2},{2,3},{4,5},{5,6},{6,7},{8,9},{9,10},{10,11},{12,13},{... | collective-permute-start | bytes 786440 | tf_op jit(solution)/shard_map/ppermute | solution.py:12
  14.3 15.1 %collective-permute-start.1 = (bf16[128,1,8,128]{3,0,2,1:T(8,128)(2,1)}, bf16[128,1,8,128]{3,0,2,1:T(8,128)(2,1)}, u32[]{:S(2)}, u32[]{:S(2)}) collective-permute-start(bf16[128,1,8,128]{3,0,2,1:T(8,128)(2,1)} %get-tuple-element.23), channel_id=1, source_target_pairs={{1,0},{2,1},{3,2},{5,4},{6,5},{7,6},{9,8},{10,9},{11,10},{13,12},{... | collective-permute-start | bytes 786440 | tf_op jit(solution)/shard_map/ppermute | solution.py:15
  15.6 5.1 %copy-start.6 = (bf16[128,2,8,128]{3,2,1,0:T(8,128)(2,1)S(1)}, bf16[128,2,8,128]{3,2,1,0:T(8,128)(2,1)}, u32[]{:S(2)}) copy-start(bf16[128,2,8,128]{3,2,1,0:T(8,128)(2,1)} %param.7) | copy-start | bytes 1572868
  25.4 3.9 %copy-start.5 = (bf16[128,2,8,128]{3,0,2,1:T(8,128)(2,1)S(1)}, bf16[128,2,8,128]{3,0,2,1:T(8,128)(2,1)}, u32[]{:S(2)}) copy-start(bf16[128,2,8,128]{3,0,2,1:T(8,128)(2,1)} %copy.18) | copy-start | bytes 1572868
  37.1 1.2 copy-start.3
  39.3 4.9 %collective-permute-start.2 = (f32[64,27,128]{2,0,1:T(8,128)}, f32[64,27,128]{2,0,1:T(8,128)}, u32[]{:S(2)}, u32[]{:S(2)}) collective-permute-start(f32[64,27,128]{2,0,1:T(8,128)} %constant_dynamic-slice_fusion.1), channel_id=1, source_target_pairs={{0,1},{1,0},{2,3},{3,2},{4,5},{5,4},{6,7},{7,6},{8,9},{9,8},{10,11... | collective-permute-start | bytes 2654216 | tf_op jit(solution)/shard_map/ppermute | solution.py:70
  45.8 22.0 %collective-permute-start.3 = (f32[64,27,128]{2,0,1:T(8,128)S(1)}, f32[64,27,128]{2,0,1:T(8,128)S(1)}, u32[]{:S(2)}, u32[]{:S(2)}) collective-permute-start(f32[64,27,128]{2,0,1:T(8,128)S(1)} %dynamic-slice_add_fusion.1), channel_id=1, source_target_pairs={{0,2},{1,3},{2,0},{3,1},{4,6},{5,7},{6,4},{7,5},{8,10},{9,11},{10,... | collective-permute-start | bytes 2654216 | tf_op jit(solution)/shard_map/ppermute | solution.py:73
  68.9 2.8 %collective-permute-start.4 = (f32[64,27,128]{2,0,1:T(8,128)}, f32[64,27,128]{2,0,1:T(8,128)}, u32[]{:S(2)}, u32[]{:S(2)}) collective-permute-start(f32[64,27,128]{2,0,1:T(8,128)} %add.58), channel_id=1, source_target_pairs={{0,1},{1,0},{2,3},{3,2},{4,5},{5,4},{6,7},{7,6},{8,9},{9,8},{10,11... | collective-permute-start | bytes 2654216 | tf_op jit(solution)/shard_map/ppermute | solution.py:78
  92.6 4.3 %collective-permute-start.5 = (bf16[512,1,8,128]{3,0,2,1:T(8,128)(2,1)}, bf16[512,1,8,128]{3,0,2,1:T(8,128)(2,1)}, u32[]{:S(2)}, u32[]{:S(2)}) collective-permute-start(bf16[512,1,8,128]{3,0,2,1:T(8,128)(2,1)} %get-tuple-element.19), channel_id=1, source_target_pairs={{0,1},{1,2},{2,3},{4,5},{5,6},{6,7},{8,9},{9,10},{10,11},{12,13},{... | collective-permute-start | bytes 3145736 | tf_op jit(solution)/shard_map/ppermute | solution.py:12
  95.3 5.2 %collective-permute-start.6 = (bf16[512,1,8,128]{3,0,2,1:T(8,128)(2,1)}, bf16[512,1,8,128]{3,0,2,1:T(8,128)(2,1)}, u32[]{:S(2)}, u32[]{:S(2)}) collective-permute-start(bf16[512,1,8,128]{3,0,2,1:T(8,128)(2,1)} %get-tuple-element.18), channel_id=1, source_target_pairs={{1,0},{2,1},{3,2},{5,4},{6,5},{7,6},{9,8},{10,9},{11,10},{13,12},{... | collective-permute-start | bytes 3145736 | tf_op jit(solution)/shard_map/ppermute | solution.py:15
  101.9 6.8 %copy-start.2 = (bf16[512,4,8,128]{3,0,2,1:T(8,128)(2,1)}, bf16[512,4,8,128]{3,0,2,1:T(8,128)(2,1)S(1)}, u32[]{:S(2)}) copy-start(bf16[512,4,8,128]{3,0,2,1:T(8,128)(2,1)S(1)} %constant_dynamic-update-slice_fusion) | copy-start | bytes 12582916
  118.5 16.7 %collective-permute-start.7 = (f32[64,27,384]{2,0,1:T(8,128)S(1)}, f32[64,27,384]{2,0,1:T(8,128)S(1)}, u32[]{:S(2)}, u32[]{:S(2)}) collective-permute-start(f32[64,27,384]{2,0,1:T(8,128)S(1)} %constant_dynamic-slice_fusion), channel_id=1, source_target_pairs={{0,1},{1,0},{2,3},{3,2},{4,5},{5,4},{6,7},{7,6},{8,9},{9,8},{10,11... | collective-permute-start | bytes 7962632 | tf_op jit(solution)/shard_map/ppermute | solution.py:70
  137.1 60.2 %collective-permute-start.8 = (f32[64,27,384]{2,0,1:T(8,128)}, f32[64,27,384]{2,0,1:T(8,128)}, u32[]{:S(2)}, u32[]{:S(2)}) collective-permute-start(f32[64,27,384]{2,0,1:T(8,128)} %dynamic-slice_add_fusion), channel_id=1, source_target_pairs={{0,2},{1,3},{2,0},{3,1},{4,6},{5,7},{6,4},{7,5},{8,10},{9,11},{10,... | collective-permute-start | bytes 7962632 | tf_op jit(solution)/shard_map/ppermute | solution.py:73
  149.1 1.9 copy-start.8
  150.9 17.1 %copy-start.7 = (f32[128]{0:T(128)S(1)}, f32[128]{0:T(128)}, u32[]{:S(2)}) copy-start(f32[128]{0:T(128)} %param.6) | copy-start | bytes 1540
  200.2 5.2 %collective-permute-start.9 = (f32[64,27,384]{2,0,1:T(8,128)S(1)}, f32[64,27,384]{2,0,1:T(8,128)}, u32[]{:S(2)}, u32[]{:S(2)}) collective-permute-start(f32[64,27,384]{2,0,1:T(8,128)S(1)} %add.64), channel_id=1, source_target_pairs={{0,1},{1,0},{2,3},{3,2},{4,5},{5,4},{6,7},{7,6},{8,9},{9,8},{10,11... | collective-permute-start | bytes 7962632 | tf_op jit(solution)/shard_map/ppermute | solution.py:78
  201.7 5.9 %copy-start.4 = (f32[128,27,128]{2,0,1:T(8,128)S(1)}, f32[128,27,128]{2,0,1:T(8,128)}, u32[]{:S(2)}) copy-start(f32[128,27,128]{2,0,1:T(8,128)} %pad_maximum_fusion.2) | copy-start | bytes 5308420
  207.5 4.6 %copy-start.1 = (bf16[128,27,512]{2,0,1:T(8,128)(2,1)S(1)}, bf16[128,27,512]{2,0,1:T(8,128)(2,1)}, u32[]{:S(2)}) copy-start(bf16[128,27,512]{2,0,1:T(8,128)(2,1)} %param.5) | copy-start | bytes 10616836
Sparse Core Ops, SparseCore 0:
  42.0 47.4 all-gather.1

commit v3 on v2

--- a/solution.py
+++ b/solution.py
@@ -55,9 +55,32 @@
     return jnp.concatenate(rows, axis=1)
 
 
-def space_sum(grads, beside=None, operand=None):
+def line_gather(block, axis):
+    count = lax.axis_size(axis)
+    here = lax.axis_index(axis)
+    lefts, rights = [], []
+    from_left = block
+    from_right = block
+    for step in range(1, count):
+        from_left = lax.ppermute(
+            from_left, axis, [(i, i + 1) for i in range(step - 1, count - 1)]
+        )
+        from_right = lax.ppermute(
+            from_right, axis, [(i, i - 1) for i in range(1, count - step + 1)]
+        )
+        lefts.append(from_left)
+        rights.append(from_right)
+    blocks = [block]
+    for k in range(1, count):
+        blocks.append(jnp.where(here + k < count, rights[k - 1], lefts[count - k - 1]))
+    return jnp.concatenate(blocks, axis=0)
+
+
+def space_sum(grads, beside=None, operand=None, tie=None):
     count = lax.axis_size("space")
     if count != 4 or grads.shape[0] % 2:
+        if tie is not None:
+            return lax.psum(grads, "space"), tie
         if beside is None:
             return lax.psum(grads, "space")
         return lax.psum(grads, "space"), beside(operand)
@@ -68,6 +91,8 @@
     mine = lax.dynamic_slice_in_dim(grads, core * half, half, axis=0)
     other = lax.dynamic_slice_in_dim(grads, (1 - core) * half, half, axis=0)
     mine = mine + lax.ppermute(other, "space", pair)
+    if tie is not None:
+        mine, tie = lax.optimization_barrier((mine, tie))
     if beside is not None:
         mine, operand = lax.optimization_barrier((mine, operand))
     arrived = lax.ppermute(mine, "space", across)
@@ -79,6 +104,8 @@
     low = jnp.where(core == 0, mine, theirs)
     high = jnp.where(core == 0, theirs, mine)
     summed = jnp.concatenate([low, high], axis=0)
+    if tie is not None:
+        return summed, tie
     if beside is None:
         return summed
     return summed, result
@@ -92,12 +119,11 @@
     kernel = weight.reshape(out_dev, 3, 3, 3, in_all).transpose(0, 4, 1, 2, 3)
     shifted = plane_shifts(upstream)
     own = padded(volume, (("space", 1),), 1)
-    own_grads = space_sum(tap_grads(own, shifted, out_dev, depth))
-    whole = lax.all_gather(volume, "filt", axis=0, tiled=True)
-    whole, own_grads = lax.optimization_barrier((whole, own_grads))
-    rimmed = padded(whole, (("space", 1),), 1)
+    rolled = line_gather(volume, "filt")
+    own_grads, rolled = space_sum(tap_grads(own, shifted, out_dev, depth), tie=rolled)
+    rolled = padded(rolled, (("space", 1),), 1)
     start = lax.axis_index("filt") * in_dev
-    rolled = jnp.roll(rimmed, -start, axis=0)
+    rimmed = jnp.roll(rolled, start, axis=0)
     rest = lax.slice_in_dim(rolled, in_dev, in_all, axis=0)
 
     def forward(slab):

time: 220 us -> 218 us (level)
  between operations: 14.4 us -> 1.06 us
  other arithmetic: 20.2 us -> 30.7 us
  starting transfers between devices: 26.7 us -> 30.8 us
    ppermute x0 -> x6, waiting for transfers between devices: none -> 22.7 us  [the longest x3 22.7 us: line_gather(): lax.ppermute(from_right, axis, [(i, i - 1) for i in range(1, count - step...]
    all_gather x1 -> x0, waiting for transfers between devices: 15 us -> none  [on_device(): whole = lax.all_gather(volume, 'filt', axis=0, tiled=True)]
    ppermute x0 -> x6, starting transfers between devices: none -> 12.4 us  [the longest x3 8.53 us: line_gather(): lax.ppermute(from_left, axis, [(i, i + 1) for i in range(step - 1, count...]
    ppermute x2, waiting for transfers between devices: 6.95 us -> 0.01 us  [space_sum(): mine = mine + lax.ppermute(other, 'space', pair)]
    ppermute x2, starting transfers between devices: 14.7 us -> 8.38 us  [space_sum(): mine = mine + lax.ppermute(other, 'space', pair)]
    ppermute x2, waiting for transfers between devices: 6.48 us -> 2.64 us  [space_sum(): theirs = lax.ppermute(mine, 'space', pair)]
    ppermute x2, starting transfers between devices: 3.65 us -> 0.35 us  [space_sum(): arrived = lax.ppermute(mine, 'space', across)]
    concatenate x2, other arithmetic: 3.56 us -> 6.74 us  [the longest x1 5.5 us: on_device(): rimmed = jnp.roll(rolled, start, axis=0)]
  transfers between devices with their start and end apart: 11 -> 16, of which waited for: 9 -> 5; matrix products, arithmetic and copies ran while one was open for 26% -> 36% of each run, Pallas kernels for 0% -> 0%
where the time goes in v3:
time: 218 us; the launch traced here: 217 us
  waiting for transfers between devices  76.5 us (35%)
  matrix products  42.4 us (19%)
  local copies, waits for them, and re-layouts  36.1 us (17%)
  starting transfers between devices  30.8 us (14%)
  other arithmetic  30.7 us (14%)
    ppermute x2, waiting for transfers between devices, space_sum(): arrived = lax.ppermute(mine, 'space', across)  51.1 us
    unnamed x40, local copies, waits for them, and re-layouts  25.8 us
    dot_general x6, matrix products, tap_grads(): lax.dot_general(shifted, flat, (((1,), (1,)), ((), ())), preferred_elemen...  25.4 us
    ppermute x3, waiting for transfers between devices, line_gather(): lax.ppermute(from_right, axis, [(i, i - 1) for i in range(1, count - step...  22.7 us
    conv_general_dilated x1, matrix products, convolve(): lax.conv_general_dilated(slab[None], kernel, (1, 1, 1), [(0, 0), (1, 1),...  16.9 us
    ppermute x3, starting transfers between devices, line_gather(): lax.ppermute(from_left, axis, [(i, i + 1) for i in range(step - 1, count...  8.53 us
    ppermute x2, starting transfers between devices, space_sum(): mine = mine + lax.ppermute(other, 'space', pair)  8.38 us
    ppermute x2, starting transfers between devices, padded(): lax.ppermute(lax.slice_in_dim(block, block.shape[dim] - width, None, axis...  7.04 us
  transfers between devices with their start and end apart: 16, of which 5 were waited for; matrix products, arithmetic and copies ran while one was open for 36% of the time, Pallas kernels for 0%

profile of v3, /device:TPU:0, one launch (start us, length us, event | category | flops | bytes accessed | tf_op | source)
XLA Modules:
  0.0 217.5 jit_solution(1266621889014079624)
XLA Ops:
  4.1 6.4 %collective-permute-start.4 = (bf16[128,2,8,128]{3,0,2,1:T(8,128)(2,1)}, bf16[128,2,8,128]{3,0,2,1:T(8,128)(2,1)}, u32[]{:S(2)}, u32[]{:S(2)}) collective-permute-start(bf16[128,2,8,128]{3,0,2,1:T(8,128)(2,1)} %copy.20), channel_id=1, source_target_pairs={{0,4},{4,8},{8,12},{1,5},{5,9},{9,13},{2,6},{6,10},{10,14},{3,7},{... | collective-permute-start | bytes 1572872 | tf_op jit(solution)/shard_map/ppermute | solution.py:65
  13.6 3.8 %collective-permute-start = (bf16[128,1,8,128]{3,0,2,1:T(8,128)(2,1)}, bf16[128,1,8,128]{3,0,2,1:T(8,128)(2,1)}, u32[]{:S(2)}, u32[]{:S(2)}) collective-permute-start(bf16[128,1,8,128]{3,0,2,1:T(8,128)(2,1)} %get-tuple-element.22), channel_id=1, source_target_pairs={{0,1},{1,2},{2,3},{4,5},{5,6},{6,7},{8,9},{9,10},{10,11},{12,13},{... | collective-permute-start | bytes 786440 | tf_op jit(solution)/shard_map/ppermute | solution.py:12
  27.2 3.9 %convolution_bitcast_fusion.1 = f32[128,9,128]{2,0,1:T(8,128)S(1)} fusion(bf16[128,9,2,8,128]{4,0,3,2,1:T(8,128)(2,1)} %fusion.61, bf16[128,2,8,128,1]{3,2,1,0,4:T(8,128)(2,1)} %bitcast.143), kind=kOutput, calls=%fused_computation.66 | convolution fusion | flops 603979776 | bytes 5832704 | tf_op jit(solution)/shard_map/dot_general | solution.py:51
  31.1 3.8 %convolution_bitcast_fusion = f32[128,9,128]{2,0,1:T(8,128)S(1)} fusion(bf16[128,9,2,8,128]{4,0,3,2,1:T(8,128)(2,1)} %fusion.61, bf16[128,1,8,128]{3,0,2,1:T(8,128)(2,1)} %collective-permute-done.1, bf16[128,2,8,128]{3,0,2,1:T(8,128)(2,1)} %copy.20), kind=kOutput, calls=%fused_computation.65 | convolution fusion | flops 604241920 | bytes 6094848 | tf_op jit(solution)/shard_map/dot_general | solution.py:51
  34.9 3.8 %convolution_bitcast_fusion.2 = f32[128,9,128]{2,0,1:T(8,128)S(1)} fusion(bf16[128,9,2,8,128]{4,0,3,2,1:T(8,128)(2,1)} %fusion.61, bf16[128,2,8,128]{3,0,2,1:T(8,128)(2,1)} %copy.20, bf16[128,1,8,128]{3,0,2,1:T(8,128)(2,1)} %collective-permute-done), kind=kOutput, calls=%fused_computation.67 | convolution fusion | flops 604241920 | bytes 6094848 | tf_op jit(solution)/shard_map/dot_general | solution.py:51
  44.8 13.3 %collective-permute-done.7 = bf16[128,2,8,128]{3,0,2,1:T(8,128)(2,1)} collective-permute-done((bf16[128,2,8,128]{3,0,2,1:T(8,128)(2,1)}, bf16[128,2,8,128]{3,0,2,1:T(8,128)(2,1)}, u32[]{:S(2)}, u32[]{:S(2)}) %collective-permute-start.7) | collective-permute-done | bytes 524320 | tf_op jit(solution)/shard_map/ppermute | solution.py:68
  61.1 2.5 %dynamic-slice_add_fusion.1 = f32[64,27,128]{2,0,1:T(8,128)} fusion(f32[64,27,128]{2,0,1:T(8,128)} %collective-permute-done.2, f32[128,27,128]{2,0,1:T(8,128)} %copy-done.5, s32[]{:T(128)S(6)} %select_n.84), kind=kLoop, calls=%fused_computation.71 | loop fusion | flops 221184 | bytes 2654212 | tf_op jit(solution)/shard_map/add | solution.py:93
  63.7 9.4 %collective-permute-done.8 = bf16[128,2,8,128]{3,0,2,1:T(8,128)(2,1)S(1)} collective-permute-done((bf16[128,2,8,128]{3,0,2,1:T(8,128)(2,1)}, bf16[128,2,8,128]{3,0,2,1:T(8,128)(2,1)S(1)}, u32[]{:S(2)}, u32[]{:S(2)}) %collective-permute-start.8) | collective-permute-done | bytes 524320 | tf_op jit(solution)/shard_map/ppermute | solution.py:68
  77.0 3.3 %collective-permute-start.9 = (bf16[512,1,8,128]{3,0,2,1:T(8,128)(2,1)S(1)}, bf16[512,1,8,128]{3,0,2,1:T(8,128)(2,1)S(1)}, u32[]{:S(2)}, u32[]{:S(2)}) collective-permute-start(bf16[512,1,8,128]{3,0,2,1:T(8,128)(2,1)S(1)} %get-tuple-element.18), channel_id=1, source_target_pairs={{0,1},{1,2},{2,3},{4,5},{5,6},{6,7},{8,9},{9,10},{10,11},{12,13},{... | collective-permute-start | bytes 3145736 | tf_op jit(solution)/shard_map/ppermute | solution.py:12
  80.3 4.5 %fusion.32 = f32[128,9,384]{2,0,1:T(8,128)S(1)} fusion(bf16[128,9,2,8,128]{4,0,3,2,1:T(8,128)(2,1)} %fusion.61, bf16[512,2,8,128]{3,0,2,1:T(8,128)(2,1)S(1)} %pad_maximum_fusion.1), kind=kOutput, calls=%fused_computation.59 | convolution fusion | flops 1811939328 | bytes 8060928 | tf_op jit(solution)/shard_map/dot_general | solution.py:51
  84.8 4.9 %fusion.38 = f32[128,9,384]{2,0,1:T(8,128)S(1)} fusion(bf16[128,9,2,8,128]{4,0,3,2,1:T(8,128)(2,1)} %fusion.61, bf16[512,1,8,128]{3,0,2,1:T(8,128)(2,1)S(1)} %collective-permute-done.10, bf16[512,2,8,128]{3,0,2,1:T(8,128)(2,1)S(1)} %pad_maximum_fusion.1), kind=kOutput, calls=%fused_computation.61 | convolution fusion | flops 1815085056 | bytes 9633792 | tf_op jit(solution)/shard_map/dot_general | solution.py:51
  90.8 4.5 %fusion.35 = f32[128,9,384]{2,0,1:T(8,128)S(1)} fusion(bf16[128,9,2,8,128]{4,0,3,2,1:T(8,128)(2,1)} %fusion.61, bf16[512,2,8,128]{3,0,2,1:T(8,128)(2,1)S(1)} %pad_maximum_fusion.1, bf16[512,1,8,128]{3,0,2,1:T(8,128)(2,1)S(1)} %collective-permute-done.9), kind=kOutput, calls=%fused_computation.60 | convolution fusion | flops 1815085056 | bytes 9633792 | tf_op jit(solution)/shard_map/dot_general | solution.py:51
  100.0 7.5 %collective-permute-start.11 = (f32[64,27,384]{2,0,1:T(8,128)}, f32[64,27,384]{2,0,1:T(8,128)}, u32[]{:S(2)}, u32[]{:S(2)}) collective-permute-start(f32[64,27,384]{2,0,1:T(8,128)} %constant_dynamic-slice_fusion), channel_id=1, source_target_pairs={{0,1},{1,0},{2,3},{3,2},{4,5},{5,4},{6,7},{7,6},{8,9},{9,8},{10,11... | collective-permute-start | bytes 7962632 | tf_op jit(solution)/shard_map/ppermute | solution.py:93
  107.5 5.5 %fusion.17 = bf16[512,4,8,128]{3,0,2,1:T(8,128)(2,1)} fusion(s32[]{:T(128)S(6)} %select_n.93, bf16[512,1,8,128]{3,0,2,1:T(8,128)(2,1)} %copy-done.11, bf16[512,2,8,128]{3,0,2,1:T(8,128)(2,1)} %copy-done.4, bf16[512,1,8,128]{3,0,2,1:T(8,128)(2,1)} %copy-done.10), kind=kLoop, calls=%fused_computation.32 | loop fusion | flops 25165824 | bytes 8388612 | tf_op jit(solution)/shard_map/jit(_roll_dynamic)/concatenate | solution.py:126
  113.1 3.7 %dynamic-slice_add_fusion = f32[64,27,384]{2,0,1:T(8,128)} fusion(f32[64,27,384]{2,0,1:T(8,128)} %collective-permute-done.11, f32[128,27,384]{2,0,1:T(8,128)S(1)} %copy-done.3, s32[]{:T(128)S(6)} %select_n.84), kind=kLoop, calls=%fused_computation.44 | loop fusion | flops 663552 | bytes 7962628 | tf_op jit(solution)/shard_map/add | solution.py:93
  116.8 7.8 %copy.48 = bf16[512,4,8,1,128]{0,2,4,1,3:T(8,128)(2,1)} copy(bf16[512,4,8,1,128]{4,0,2,1,3:T(8,128)(2,1)} %bitcast.141) | data formatting | bytes 8388608
  124.6 2.5 %pad.5.clone = bf16[512,4,8,1,136]{0,2,4,1,3:T(8,128)(2,1)S(1)} pad(bf16[512,4,8,1,128]{0,2,4,1,3:T(8,128)(2,1)} %copy.48, bf16[]{:T(256)} %constant.54.clone.1), padding=0_0x0_0x0_0x0_0x1_7 | pad | bytes 8650754 | tf_op jit(solution)/shard_map/broadcast_in_dim | solution.py:22
  129.1 16.9 %fusion.41 = f32[2,8,8,17,128]{4,2,3,1,0:T(8,128)S(1)} fusion(bf16[128,3,3,3,512]{4,0,3,2,1:T(8,128)(2,1)S(1)} %bitcast.139, bf16[512,4,8,1,7,2]{0,4,5,2,1,3:T(8,128)(2,1)S(1)} %slice.82, bf16[512,4,8,1,8,17]{0,4,5,2,1,3:T(8,128)(2,1)S(1)} %copy.30, pred[8,17]{0,1:T(8,128)(4,1)S(1)} %copy-done.13), kind=kOutput, calls=%fused_computation.64 | convolution fusion | flops 7074234368 | bytes 9568392 | tf_op jit(solution)/shard_map/conv_general_dilated | solution.py:21
  147.2 29.4 %collective-permute-done.12 = f32[64,27,384]{2,0,1:T(8,128)} collective-permute-done((f32[64,27,384]{2,0,1:T(8,128)}, f32[64,27,384]{2,0,1:T(8,128)}, u32[]{:S(2)}, u32[]{:S(2)}) %collective-permute-start.12) | collective-permute-done | bytes 2654240 | tf_op jit(solution)/shard_map/ppermute | solution.py:98
  176.6 3.0 %add.71 = f32[64,27,384]{2,0,1:T(8,128)S(1)} add(f32[64,27,384]{2,0,1:T(8,128)} %dynamic-slice_add_fusion, f32[64,27,384]{2,0,1:T(8,128)} %collective-permute-done.12) | non-fusion elementwise | flops 663552 | bytes 7962624 | tf_op jit(solution)/shard_map/add | solution.py:102
  180.0 21.7 %collective-permute-done.13 = f32[64,27,128]{2,0,1:T(8,128)S(1)} collective-permute-done((f32[64,27,128]{2,0,1:T(8,128)S(1)}, f32[64,27,128]{2,0,1:T(8,128)S(1)}, u32[]{:S(2)}, u32[]{:S(2)}) %collective-permute-start.13) | collective-permute-done | bytes 884768 | tf_op jit(solution)/shard_map/ppermute | solution.py:98
  202.7 2.6 %collective-permute-done.14 = f32[64,27,128]{2,0,1:T(8,128)S(1)} collective-permute-done((f32[64,27,128]{2,0,1:T(8,128)}, f32[64,27,128]{2,0,1:T(8,128)S(1)}, u32[]{:S(2)}, u32[]{:S(2)}) %collective-permute-start.14) | collective-permute-done | bytes 884768 | tf_op jit(solution)/shard_map/ppermute | solution.py:103
  205.4 2.6 %broadcast_select_fusion.5 = (f32[64,27,128]{2,0,1:T(8,128)}, f32[64,27,128]{2,0,1:T(8,128)}) fusion(f32[64,27,128]{2,0,1:T(8,128)S(1)} %collective-permute-done.14, f32[64,27,128]{2,0,1:T(8,128)} %add.70, pred[]{:T(512)S(6)} %eq.14), kind=kLoop, calls=%fused_computation.100 | loop fusion | flops 442368 | bytes 3538945 | tf_op jit(solution)/shard_map/jit(_where)/select_n | solution.py:105
  212.7 4.8 %fusion.4 = f32[128,27,512]{2,0,1:T(8,128)} fusion(s32[]{:T(128)S(6)} %select_n.93, f32[64,27,128]{2,0,1:T(8,128)S(1)} %copy-done.8, f32[64,27,128]{2,0,1:T(8,128)S(1)} %copy-done.7, f32[64,27,384]{2,0,1:T(8,128)S(1)} %get-tuple-element.17, f32[64,27,384]{2,0,1:T(8,128)S(1)} %get-tuple-element.16), kind=kLoop, calls=%fused_computation.19 | loop fusion | flops 12386304 | bytes 14155780 | tf_op jit(solution)/shard_map/jit(_roll_dynamic)/concatenate | solution.py:134
  (79 shorter events, 44.2 us)
Async XLA Ops:
  0.6 128.4 %copy-start = (bf16[128,27,512]{2,0,1:T(8,128)(2,1)S(1)}, bf16[128,27,512]{2,0,1:T(8,128)(2,1)}, u32[]{:S(2)}) copy-start(bf16[128,27,512]{2,0,1:T(8,128)(2,1)} %param.5) | copy-start | bytes 10616836
  2.8 39.2 %collective-permute-start.3 = (bf16[128,2,8,128]{3,0,2,1:T(8,128)(2,1)}, bf16[128,2,8,128]{3,0,2,1:T(8,128)(2,1)}, u32[]{:S(2)}, u32[]{:S(2)}) collective-permute-start(bf16[128,2,8,128]{3,0,2,1:T(8,128)(2,1)} %copy.20), channel_id=1, source_target_pairs={{4,0},{8,4},{12,8},{5,1},{9,5},{13,9},{6,2},{10,6},{14,10},{7,3},{... | collective-permute-start | bytes 1572872 | tf_op jit(solution)/shard_map/ppermute | solution.py:68
  4.1 39.2 %collective-permute-start.4 = (bf16[128,2,8,128]{3,0,2,1:T(8,128)(2,1)}, bf16[128,2,8,128]{3,0,2,1:T(8,128)(2,1)}, u32[]{:S(2)}, u32[]{:S(2)}) collective-permute-start(bf16[128,2,8,128]{3,0,2,1:T(8,128)(2,1)} %copy.20), channel_id=1, source_target_pairs={{0,4},{4,8},{8,12},{1,5},{5,9},{9,13},{2,6},{6,10},{10,14},{3,7},{... | collective-permute-start | bytes 1572872 | tf_op jit(solution)/shard_map/ppermute | solution.py:65
  12.3 18.8 %collective-permute-start.1 = (bf16[128,1,8,128]{3,0,2,1:T(8,128)(2,1)}, bf16[128,1,8,128]{3,0,2,1:T(8,128)(2,1)}, u32[]{:S(2)}, u32[]{:S(2)}) collective-permute-start(bf16[128,1,8,128]{3,0,2,1:T(8,128)(2,1)} %get-tuple-element.23), channel_id=1, source_target_pairs={{1,0},{2,1},{3,2},{5,4},{6,5},{7,6},{9,8},{10,9},{11,10},{13,12},{... | collective-permute-start | bytes 786440 | tf_op jit(solution)/shard_map/ppermute | solution.py:15
  13.6 21.3 %collective-permute-start = (bf16[128,1,8,128]{3,0,2,1:T(8,128)(2,1)}, bf16[128,1,8,128]{3,0,2,1:T(8,128)(2,1)}, u32[]{:S(2)}, u32[]{:S(2)}) collective-permute-start(bf16[128,1,8,128]{3,0,2,1:T(8,128)(2,1)} %get-tuple-element.22), channel_id=1, source_target_pairs={{0,1},{1,2},{2,3},{4,5},{5,6},{6,7},{8,9},{9,10},{10,11},{12,13},{... | collective-permute-start | bytes 786440 | tf_op jit(solution)/shard_map/ppermute | solution.py:12
  17.3 5.1 %copy-start.9 = (bf16[128,2,8,128]{3,2,1,0:T(8,128)(2,1)S(1)}, bf16[128,2,8,128]{3,2,1,0:T(8,128)(2,1)}, u32[]{:S(2)}) copy-start(bf16[128,2,8,128]{3,2,1,0:T(8,128)(2,1)} %param.7) | copy-start | bytes 1572868
  41.1 20.0 %collective-permute-start.2 = (f32[64,27,128]{2,0,1:T(8,128)}, f32[64,27,128]{2,0,1:T(8,128)}, u32[]{:S(2)}, u32[]{:S(2)}) collective-permute-start(f32[64,27,128]{2,0,1:T(8,128)} %constant_dynamic-slice_fusion.1), channel_id=1, source_target_pairs={{0,1},{1,0},{2,3},{3,2},{4,5},{5,4},{6,7},{7,6},{8,9},{9,8},{10,11... | collective-permute-start | bytes 2654216 | tf_op jit(solution)/shard_map/ppermute | solution.py:93
  42.0 16.0 %collective-permute-start.7 = (bf16[128,2,8,128]{3,0,2,1:T(8,128)(2,1)}, bf16[128,2,8,128]{3,0,2,1:T(8,128)(2,1)}, u32[]{:S(2)}, u32[]{:S(2)}) collective-permute-start(bf16[128,2,8,128]{3,0,2,1:T(8,128)(2,1)} %collective-permute-done.3), channel_id=1, source_target_pairs={{4,0},{8,4},{5,1},{9,5},{6,2},{10,6},{7,3},{11,7},{20,16},{24,20},... | collective-permute-start | bytes 1572872 | tf_op jit(solution)/shard_map/ppermute | solution.py:68
  43.3 16.0 %collective-permute-start.5 = (bf16[128,2,8,128]{3,0,2,1:T(8,128)(2,1)}, bf16[128,2,8,128]{3,0,2,1:T(8,128)(2,1)}, u32[]{:S(2)}, u32[]{:S(2)}) collective-permute-start(bf16[128,2,8,128]{3,0,2,1:T(8,128)(2,1)} %collective-permute-done.4), channel_id=1, source_target_pairs={{4,8},{8,12},{5,9},{9,13},{6,10},{10,14},{7,11},{11,15},{20,24},{2... | collective-permute-start | bytes 1572872 | tf_op jit(solution)/shard_map/ppermute | solution.py:65
  58.0 15.1 %collective-permute-start.8 = (bf16[128,2,8,128]{3,0,2,1:T(8,128)(2,1)}, bf16[128,2,8,128]{3,0,2,1:T(8,128)(2,1)S(1)}, u32[]{:S(2)}, u32[]{:S(2)}) collective-permute-start(bf16[128,2,8,128]{3,0,2,1:T(8,128)(2,1)} %collective-permute-done.7), channel_id=1, source_target_pairs={{4,0},{5,1},{6,2},{7,3},{20,16},{21,17},{22,18},{23,19}} | collective-permute-start | bytes 1572872 | tf_op jit(solution)/shard_map/ppermute | solution.py:68
  59.3 13.8 %collective-permute-start.6 = (bf16[128,2,8,128]{3,0,2,1:T(8,128)(2,1)}, bf16[128,2,8,128]{3,0,2,1:T(8,128)(2,1)S(1)}, u32[]{:S(2)}, u32[]{:S(2)}) collective-permute-start(bf16[128,2,8,128]{3,0,2,1:T(8,128)(2,1)} %collective-permute-done.5), channel_id=1, source_target_pairs={{8,12},{9,13},{10,14},{11,15},{24,28},{25,29},{26,30},{27,31}} | collective-permute-start | bytes 1572872 | tf_op jit(solution)/shard_map/ppermute | solution.py:65
  75.5 14.2 %copy-start.4 = (bf16[512,2,8,128]{3,0,2,1:T(8,128)(2,1)}, bf16[512,2,8,128]{3,0,2,1:T(8,128)(2,1)S(1)}, u32[]{:S(2)}) copy-start(bf16[512,2,8,128]{3,0,2,1:T(8,128)(2,1)S(1)} %pad_maximum_fusion.1) | copy-start | bytes 6291460
  75.7 9.1 %collective-permute-start.10 = (bf16[512,1,8,128]{3,0,2,1:T(8,128)(2,1)S(1)}, bf16[512,1,8,128]{3,0,2,1:T(8,128)(2,1)S(1)}, u32[]{:S(2)}, u32[]{:S(2)}) collective-permute-start(bf16[512,1,8,128]{3,0,2,1:T(8,128)(2,1)S(1)} %get-tuple-element.19), channel_id=1, source_target_pairs={{1,0},{2,1},{3,2},{5,4},{6,5},{7,6},{9,8},{10,9},{11,10},{13,12},{... | collective-permute-start | bytes 3145736 | tf_op jit(solution)/shard_map/ppermute | solution.py:15
  77.0 12.7 %collective-permute-start.9 = (bf16[512,1,8,128]{3,0,2,1:T(8,128)(2,1)S(1)}, bf16[512,1,8,128]{3,0,2,1:T(8,128)(2,1)S(1)}, u32[]{:S(2)}, u32[]{:S(2)}) collective-permute-start(bf16[512,1,8,128]{3,0,2,1:T(8,128)(2,1)S(1)} %get-tuple-element.18), channel_id=1, source_target_pairs={{0,1},{1,2},{2,3},{4,5},{5,6},{6,7},{8,9},{9,10},{10,11},{12,13},{... | collective-permute-start | bytes 3145736 | tf_op jit(solution)/shard_map/ppermute | solution.py:12
  84.8 4.9 %copy-start.10 = (bf16[512,1,8,128]{3,0,2,1:T(8,128)(2,1)}, bf16[512,1,8,128]{3,0,2,1:T(8,128)(2,1)S(1)}, u32[]{:S(2)}) copy-start(bf16[512,1,8,128]{3,0,2,1:T(8,128)(2,1)S(1)} %collective-permute-done.10) | copy-start | bytes 3145732
  100.0 13.0 %collective-permute-start.11 = (f32[64,27,384]{2,0,1:T(8,128)}, f32[64,27,384]{2,0,1:T(8,128)}, u32[]{:S(2)}, u32[]{:S(2)}) collective-permute-start(f32[64,27,384]{2,0,1:T(8,128)} %constant_dynamic-slice_fusion), channel_id=1, source_target_pairs={{0,1},{1,0},{2,3},{3,2},{4,5},{5,4},{6,7},{7,6},{8,9},{9,8},{10,11... | collective-permute-start | bytes 7962632 | tf_op jit(solution)/shard_map/ppermute | solution.py:93
  107.5 5.5 %copy-start.3 = (f32[128,27,384]{2,0,1:T(8,128)S(1)}, f32[128,27,384]{2,0,1:T(8,128)}, u32[]{:S(2)}) copy-start(f32[128,27,384]{2,0,1:T(8,128)} %copy-done.2) | copy-start | bytes 15925252
  116.8 59.8 %collective-permute-start.12 = (f32[64,27,384]{2,0,1:T(8,128)}, f32[64,27,384]{2,0,1:T(8,128)}, u32[]{:S(2)}, u32[]{:S(2)}) collective-permute-start(f32[64,27,384]{2,0,1:T(8,128)} %dynamic-slice_add_fusion), channel_id=1, source_target_pairs={{0,2},{1,3},{2,0},{3,1},{4,6},{5,7},{6,4},{7,5},{8,10},{9,11},{10,... | collective-permute-start | bytes 7962632 | tf_op jit(solution)/shard_map/ppermute | solution.py:98
  129.0 17.2 %copy-start.12 = (f32[128]{0:T(128)S(1)}, f32[128]{0:T(128)}, u32[]{:S(2)}) copy-start(f32[128]{0:T(128)} %param.6) | copy-start | bytes 1540
  146.2 33.4 %copy-start.6 = (f32[64,27,128]{2,0,1:T(8,128)S(1)}, f32[64,27,128]{2,0,1:T(8,128)}, u32[]{:S(2)}) copy-start(f32[64,27,128]{2,0,1:T(8,128)} %dynamic-slice_add_fusion.1) | copy-start | bytes 2654212
  179.6 30.8 %collective-permute-start.15 = (f32[64,27,384]{2,0,1:T(8,128)S(1)}, f32[64,27,384]{2,0,1:T(8,128)}, u32[]{:S(2)}, u32[]{:S(2)}) collective-permute-start(f32[64,27,384]{2,0,1:T(8,128)S(1)} %add.71), channel_id=1, source_target_pairs={{0,1},{1,0},{2,3},{3,2},{4,5},{5,4},{6,7},{7,6},{8,9},{9,8},{10,11... | collective-permute-start | bytes 7962632 | tf_op jit(solution)/shard_map/ppermute | solution.py:103
  179.7 22.1 %collective-permute-start.13 = (f32[64,27,128]{2,0,1:T(8,128)S(1)}, f32[64,27,128]{2,0,1:T(8,128)S(1)}, u32[]{:S(2)}, u32[]{:S(2)}) collective-permute-start(f32[64,27,128]{2,0,1:T(8,128)S(1)} %copy-done.6), channel_id=1, source_target_pairs={{0,2},{1,3},{2,0},{3,1},{4,6},{5,7},{6,4},{7,5},{8,10},{9,11},{10,... | collective-permute-start | bytes 2654216 | tf_op jit(solution)/shard_map/ppermute | solution.py:98
  202.7 2.6 %collective-permute-start.14 = (f32[64,27,128]{2,0,1:T(8,128)}, f32[64,27,128]{2,0,1:T(8,128)S(1)}, u32[]{:S(2)}, u32[]{:S(2)}) collective-permute-start(f32[64,27,128]{2,0,1:T(8,128)} %add.70), channel_id=1, source_target_pairs={{0,1},{1,0},{2,3},{3,2},{4,5},{5,4},{6,7},{7,6},{8,9},{9,8},{10,11... | collective-permute-start | bytes 2654216 | tf_op jit(solution)/shard_map/ppermute | solution.py:103
  212.6 4.8 %copy-start.1 = (bf16[128,27,512]{2,0,1:T(8,128)(2,1)S(1)}, bf16[128,27,512]{2,0,1:T(8,128)(2,1)}, u32[]{:S(2)}) copy-start(bf16[128,27,512]{2,0,1:T(8,128)(2,1)} %param.5) | copy-start | bytes 10616836
  (6 other events, 11.1 us)

commit v4 on v3

--- a/solution.py
+++ b/solution.py
@@ -91,8 +91,6 @@
     mine = lax.dynamic_slice_in_dim(grads, core * half, half, axis=0)
     other = lax.dynamic_slice_in_dim(grads, (1 - core) * half, half, axis=0)
     mine = mine + lax.ppermute(other, "space", pair)
-    if tie is not None:
-        mine, tie = lax.optimization_barrier((mine, tie))
     if beside is not None:
         mine, operand = lax.optimization_barrier((mine, operand))
     arrived = lax.ppermute(mine, "space", across)
@@ -105,7 +103,7 @@
     high = jnp.where(core == 0, theirs, mine)
     summed = jnp.concatenate([low, high], axis=0)
     if tie is not None:
-        return summed, tie
+        return lax.optimization_barrier((summed, tie))
     if beside is None:
         return summed
     return summed, result

time: 218 us -> 204 us (0.936)
  waiting for transfers between devices: 76.5 us -> 61.1 us
  starting transfers between devices: 30.8 us -> 33.2 us
    ppermute x2, waiting for transfers between devices: 51.1 us -> 30.2 us  [space_sum(): arrived = lax.ppermute(mine, 'space', across)]
    ppermute x3, waiting for transfers between devices: 22.7 us -> 27.1 us  [line_gather(): lax.ppermute(from_right, axis, [(i, i - 1) for i in range(1, count - step...]
    ppermute x2, starting transfers between devices: 8.38 us -> 11.2 us  [space_sum(): mine = mine + lax.ppermute(other, 'space', pair)]
    select_n x2 -> x1, other arithmetic: 4.9 us -> 2.16 us  [space_sum(): high = jnp.where(core == 0, theirs, mine)]
    unnamed x40 -> x36, local copies, waits for them, and re-layouts: 25.8 us -> 24.8 us
  transfers between devices with their start and end apart: 16 -> 16, of which waited for: 5 -> 5; matrix products, arithmetic and copies ran while one was open for 36% -> 35% of each run, Pallas kernels for 0% -> 0%
where the time goes in v4:
time: 204 us; the launch traced here: 203 us
  waiting for transfers between devices  61.1 us (30%)
  matrix products  42.4 us (21%)
  local copies, waits for them, and re-layouts  35.1 us (17%)
  starting transfers between devices  33.2 us (16%)
  other arithmetic  30.3 us (15%)
    ppermute x2, waiting for transfers between devices, space_sum(): arrived = lax.ppermute(mine, 'space', across)  30.2 us
    ppermute x3, waiting for transfers between devices, line_gather(): lax.ppermute(from_right, axis, [(i, i - 1) for i in range(1, count - step...  27.1 us
    dot_general x6, matrix products, tap_grads(): lax.dot_general(shifted, flat, (((1,), (1,)), ((), ())), preferred_elemen...  25.5 us
    unnamed x36, local copies, waits for them, and re-layouts  24.8 us
    conv_general_dilated x1, matrix products, convolve(): lax.conv_general_dilated(slab[None], kernel, (1, 1, 1), [(0, 0), (1, 1),...  16.9 us
    ppermute x2, starting transfers between devices, space_sum(): mine = mine + lax.ppermute(other, 'space', pair)  11.2 us
    ppermute x3, starting transfers between devices, line_gather(): lax.ppermute(from_left, axis, [(i, i + 1) for i in range(step - 1, count...  7.53 us
    ppermute x2, starting transfers between devices, padded(): lax.ppermute(lax.slice_in_dim(block, block.shape[dim] - width, None, axis...  6.34 us
  transfers between devices with their start and end apart: 16, of which 5 were waited for; matrix products, arithmetic and copies ran while one was open for 35% of the time, Pallas kernels for 0%

profile of v4, /device:TPU:0, one launch (start us, length us, event | category | flops | bytes accessed | tf_op | source)
XLA Modules:
  0.0 203.2 jit_solution(12892726092172903302)
XLA Ops:
  4.7 3.1 %collective-permute-start = (bf16[128,1,8,128]{3,0,2,1:T(8,128)(2,1)}, bf16[128,1,8,128]{3,0,2,1:T(8,128)(2,1)}, u32[]{:S(2)}, u32[]{:S(2)}) collective-permute-start(bf16[128,1,8,128]{3,0,2,1:T(8,128)(2,1)} %get-tuple-element.22), channel_id=1, source_target_pairs={{0,1},{1,2},{2,3},{4,5},{5,6},{6,7},{8,9},{9,10},{10,11},{12,13},{... | collective-permute-start | bytes 786440 | tf_op jit(solution)/shard_map/ppermute | solution.py:12
  18.9 3.9 %convolution_bitcast_fusion.1 = f32[128,9,128]{2,0,1:T(8,128)S(1)} fusion(bf16[128,9,2,8,128]{4,0,3,2,1:T(8,128)(2,1)} %fusion.59, bf16[128,2,8,128,1]{3,2,1,0,4:T(8,128)(2,1)} %bitcast.143), kind=kOutput, calls=%fused_computation.63 | convolution fusion | flops 603979776 | bytes 5832704 | tf_op jit(solution)/shard_map/dot_general | solution.py:51
  22.8 3.8 %convolution_bitcast_fusion = f32[128,9,128]{2,0,1:T(8,128)S(1)} fusion(bf16[128,9,2,8,128]{4,0,3,2,1:T(8,128)(2,1)} %fusion.59, bf16[128,1,8,128]{3,0,2,1:T(8,128)(2,1)} %collective-permute-done.1, bf16[128,2,8,128]{3,0,2,1:T(8,128)(2,1)} %copy.20), kind=kOutput, calls=%fused_computation.62 | convolution fusion | flops 604241920 | bytes 6094848 | tf_op jit(solution)/shard_map/dot_general | solution.py:51
  26.6 3.8 %convolution_bitcast_fusion.2 = f32[128,9,128]{2,0,1:T(8,128)S(1)} fusion(bf16[128,9,2,8,128]{4,0,3,2,1:T(8,128)(2,1)} %fusion.59, bf16[128,2,8,128]{3,0,2,1:T(8,128)(2,1)} %copy.20, bf16[128,1,8,128]{3,0,2,1:T(8,128)(2,1)} %collective-permute-done), kind=kOutput, calls=%fused_computation.64 | convolution fusion | flops 604241920 | bytes 6094848 | tf_op jit(solution)/shard_map/dot_general | solution.py:51
  32.9 2.5 %collective-permute-start.2 = (f32[64,27,128]{2,0,1:T(8,128)}, f32[64,27,128]{2,0,1:T(8,128)}, u32[]{:S(2)}, u32[]{:S(2)}) collective-permute-start(f32[64,27,128]{2,0,1:T(8,128)} %constant_dynamic-slice_fusion.1), channel_id=1, source_target_pairs={{0,1},{1,0},{2,3},{3,2},{4,5},{5,4},{6,7},{7,6},{8,9},{9,8},{10,11... | collective-permute-start | bytes 2654216 | tf_op jit(solution)/shard_map/ppermute | solution.py:93
  36.7 5.4 %collective-permute-start.6 = (bf16[128,2,8,128]{3,0,2,1:T(8,128)(2,1)}, bf16[128,2,8,128]{3,0,2,1:T(8,128)(2,1)}, u32[]{:S(2)}, u32[]{:S(2)}) collective-permute-start(bf16[128,2,8,128]{3,0,2,1:T(8,128)(2,1)} %copy.20), channel_id=1, source_target_pairs={{0,4},{4,8},{8,12},{1,5},{5,9},{9,13},{2,6},{6,10},{10,14},{3,7},{... | collective-permute-start | bytes 1572872 | tf_op jit(solution)/shard_map/ppermute | solution.py:65
  42.1 2.5 %dynamic-slice_add_fusion.1 = f32[64,27,128]{2,0,1:T(8,128)} fusion(f32[64,27,128]{2,0,1:T(8,128)} %collective-permute-done.2, f32[128,27,128]{2,0,1:T(8,128)} %copy-done.5, s32[]{:T(128)S(6)} %select_n.85), kind=kLoop, calls=%fused_computation.68 | loop fusion | flops 221184 | bytes 2654212 | tf_op jit(solution)/shard_map/add | solution.py:93
  46.2 5.2 %collective-permute-done.5 = bf16[128,2,8,128]{3,0,2,1:T(8,128)(2,1)} collective-permute-done((bf16[128,2,8,128]{3,0,2,1:T(8,128)(2,1)}, bf16[128,2,8,128]{3,0,2,1:T(8,128)(2,1)}, u32[]{:S(2)}, u32[]{:S(2)}) %collective-permute-start.5) | collective-permute-done | bytes 524320 | tf_op jit(solution)/shard_map/ppermute | solution.py:68
  54.2 12.4 %collective-permute-done.9 = bf16[128,2,8,128]{3,0,2,1:T(8,128)(2,1)} collective-permute-done((bf16[128,2,8,128]{3,0,2,1:T(8,128)(2,1)}, bf16[128,2,8,128]{3,0,2,1:T(8,128)(2,1)}, u32[]{:S(2)}, u32[]{:S(2)}) %collective-permute-start.9) | collective-permute-done | bytes 524320 | tf_op jit(solution)/shard_map/ppermute | solution.py:68
  71.4 9.5 %collective-permute-done.10 = bf16[128,2,8,128]{3,0,2,1:T(8,128)(2,1)} collective-permute-done((bf16[128,2,8,128]{3,0,2,1:T(8,128)(2,1)}, bf16[128,2,8,128]{3,0,2,1:T(8,128)(2,1)}, u32[]{:S(2)}, u32[]{:S(2)}) %collective-permute-start.10) | collective-permute-done | bytes 524320 | tf_op jit(solution)/shard_map/ppermute | solution.py:68
  87.6 3.3 %collective-permute-start.11 = (bf16[512,1,8,128]{3,0,2,1:T(8,128)(2,1)S(1)}, bf16[512,1,8,128]{3,0,2,1:T(8,128)(2,1)S(1)}, u32[]{:S(2)}, u32[]{:S(2)}) collective-permute-start(bf16[512,1,8,128]{3,0,2,1:T(8,128)(2,1)S(1)} %get-tuple-element.18), channel_id=1, source_target_pairs={{0,1},{1,2},{2,3},{4,5},{5,6},{6,7},{8,9},{9,10},{10,11},{12,13},{... | collective-permute-start | bytes 3145736 | tf_op jit(solution)/shard_map/ppermute | solution.py:12
  90.9 4.5 %fusion.30 = f32[128,9,384]{2,0,1:T(8,128)S(1)} fusion(bf16[128,9,2,8,128]{4,0,3,2,1:T(8,128)(2,1)} %fusion.59, bf16[512,2,8,128]{3,0,2,1:T(8,128)(2,1)S(1)} %pad_maximum_fusion.1), kind=kOutput, calls=%fused_computation.56 | convolution fusion | flops 1811939328 | bytes 8060928 | tf_op jit(solution)/shard_map/dot_general | solution.py:51
  95.4 4.9 %fusion.36 = f32[128,9,384]{2,0,1:T(8,128)S(1)} fusion(bf16[128,9,2,8,128]{4,0,3,2,1:T(8,128)(2,1)} %fusion.59, bf16[512,1,8,128]{3,0,2,1:T(8,128)(2,1)S(1)} %collective-permute-done.12, bf16[512,2,8,128]{3,0,2,1:T(8,128)(2,1)S(1)} %pad_maximum_fusion.1), kind=kOutput, calls=%fused_computation.58 | convolution fusion | flops 1815085056 | bytes 9633792 | tf_op jit(solution)/shard_map/dot_general | solution.py:51
  101.3 4.5 %fusion.33 = f32[128,9,384]{2,0,1:T(8,128)S(1)} fusion(bf16[128,9,2,8,128]{4,0,3,2,1:T(8,128)(2,1)} %fusion.59, bf16[512,2,8,128]{3,0,2,1:T(8,128)(2,1)S(1)} %pad_maximum_fusion.1, bf16[512,1,8,128]{3,0,2,1:T(8,128)(2,1)S(1)} %collective-permute-done.11), kind=kOutput, calls=%fused_computation.57 | convolution fusion | flops 1815085056 | bytes 9633792 | tf_op jit(solution)/shard_map/dot_general | solution.py:51
  110.6 8.7 %collective-permute-start.13 = (f32[64,27,384]{2,0,1:T(8,128)}, f32[64,27,384]{2,0,1:T(8,128)}, u32[]{:S(2)}, u32[]{:S(2)}) collective-permute-start(f32[64,27,384]{2,0,1:T(8,128)} %constant_dynamic-slice_fusion), channel_id=1, source_target_pairs={{0,1},{1,0},{2,3},{3,2},{4,5},{5,4},{6,7},{7,6},{8,9},{9,8},{10,11... | collective-permute-start | bytes 7962632 | tf_op jit(solution)/shard_map/ppermute | solution.py:93
  119.2 5.5 %fusion.15 = bf16[512,4,8,128]{3,0,2,1:T(8,128)(2,1)} fusion(s32[]{:T(128)S(6)} %select_n.96, bf16[512,1,8,128]{3,0,2,1:T(8,128)(2,1)} %copy-done.9, bf16[512,2,8,128]{3,0,2,1:T(8,128)(2,1)} %copy-done.4, bf16[512,1,8,128]{3,0,2,1:T(8,128)(2,1)} %copy-done.8), kind=kLoop, calls=%fused_computation.28 | loop fusion | flops 25165824 | bytes 8388612 | tf_op jit(solution)/shard_map/jit(_roll_dynamic)/concatenate | solution.py:124
  124.8 3.8 %dynamic-slice_add_fusion = f32[64,27,384]{2,0,1:T(8,128)} fusion(f32[64,27,384]{2,0,1:T(8,128)} %collective-permute-done.13, f32[128,27,384]{2,0,1:T(8,128)S(1)} %copy-done.3, s32[]{:T(128)S(6)} %select_n.85), kind=kLoop, calls=%fused_computation.40 | loop fusion | flops 663552 | bytes 7962628 | tf_op jit(solution)/shard_map/add | solution.py:93
  128.5 7.8 %copy.48 = bf16[512,4,8,1,128]{0,2,4,1,3:T(8,128)(2,1)} copy(bf16[512,4,8,1,128]{4,0,2,1,3:T(8,128)(2,1)} %bitcast.141) | data formatting | bytes 8388608
  136.3 2.5 %pad.5.clone = bf16[512,4,8,1,136]{0,2,4,1,3:T(8,128)(2,1)S(1)} pad(bf16[512,4,8,1,128]{0,2,4,1,3:T(8,128)(2,1)} %copy.48, bf16[]{:T(256)} %constant.54.clone.1), padding=0_0x0_0x0_0x0_0x1_7 | pad | bytes 8650754 | tf_op jit(solution)/shard_map/broadcast_in_dim | solution.py:22
  140.8 16.9 %fusion.39 = f32[2,8,8,17,128]{4,2,3,1,0:T(8,128)S(1)} fusion(bf16[128,3,3,3,512]{4,0,3,2,1:T(8,128)(2,1)S(1)} %bitcast.139, bf16[512,4,8,1,7,2]{0,4,5,2,1,3:T(8,128)(2,1)S(1)} %slice.82, bf16[512,4,8,1,8,17]{0,4,5,2,1,3:T(8,128)(2,1)S(1)} %copy.30, pred[8,17]{0,1:T(8,128)(4,1)S(1)} %copy-done.11), kind=kOutput, calls=%fused_computation.61 | convolution fusion | flops 7074234368 | bytes 9568392 | tf_op jit(solution)/shard_map/conv_general_dilated | solution.py:21
  158.1 30.2 %collective-permute-done.14 = f32[64,27,384]{2,0,1:T(8,128)} collective-permute-done((f32[64,27,384]{2,0,1:T(8,128)}, f32[64,27,384]{2,0,1:T(8,128)}, u32[]{:S(2)}, u32[]{:S(2)}) %collective-permute-start.14) | collective-permute-done | bytes 2654240 | tf_op jit(solution)/shard_map/ppermute | solution.py:96
  188.3 3.0 %add.71 = f32[64,27,384]{2,0,1:T(8,128)S(1)} add(f32[64,27,384]{2,0,1:T(8,128)} %dynamic-slice_add_fusion, f32[64,27,384]{2,0,1:T(8,128)} %collective-permute-done.14) | non-fusion elementwise | flops 663552 | bytes 7962624 | tf_op jit(solution)/shard_map/add | solution.py:100
  192.7 3.7 %collective-permute-done.15 = f32[64,27,384]{2,0,1:T(8,128)} collective-permute-done((f32[64,27,384]{2,0,1:T(8,128)S(1)}, f32[64,27,384]{2,0,1:T(8,128)}, u32[]{:S(2)}, u32[]{:S(2)}) %collective-permute-start.15) | collective-permute-done | bytes 2654240 | tf_op jit(solution)/shard_map/ppermute | solution.py:101
  198.6 4.6 %fusion.3 = f32[128,27,512]{2,0,1:T(8,128)} fusion(s32[]{:T(128)S(6)} %select_n.96, f32[128,27,128]{2,0,1:T(8,128)S(1)} %copy-done.6, f32[64,27,384]{2,0,1:T(8,128)S(1)} %get-tuple-element.17, f32[64,27,384]{2,0,1:T(8,128)S(1)} %get-tuple-element.16), kind=kLoop, calls=%fused_computation.16 | loop fusion | flops 8847360 | bytes 14155780 | tf_op jit(solution)/shard_map/jit(_roll_dynamic)/concatenate | solution.py:132
  (76 shorter events, 46.1 us)
Async XLA Ops:
  0.6 140.1 %copy-start = (bf16[128,27,512]{2,0,1:T(8,128)(2,1)S(1)}, bf16[128,27,512]{2,0,1:T(8,128)(2,1)}, u32[]{:S(2)}) copy-start(bf16[128,27,512]{2,0,1:T(8,128)(2,1)} %param.5) | copy-start | bytes 10616836
  4.7 21.9 %collective-permute-start = (bf16[128,1,8,128]{3,0,2,1:T(8,128)(2,1)}, bf16[128,1,8,128]{3,0,2,1:T(8,128)(2,1)}, u32[]{:S(2)}, u32[]{:S(2)}) collective-permute-start(bf16[128,1,8,128]{3,0,2,1:T(8,128)(2,1)} %get-tuple-element.22), channel_id=1, source_target_pairs={{0,1},{1,2},{2,3},{4,5},{5,6},{6,7},{8,9},{9,10},{10,11},{12,13},{... | collective-permute-start | bytes 786440 | tf_op jit(solution)/shard_map/ppermute | solution.py:12
  7.7 15.0 %collective-permute-start.1 = (bf16[128,1,8,128]{3,0,2,1:T(8,128)(2,1)}, bf16[128,1,8,128]{3,0,2,1:T(8,128)(2,1)}, u32[]{:S(2)}, u32[]{:S(2)}) collective-permute-start(bf16[128,1,8,128]{3,0,2,1:T(8,128)(2,1)} %get-tuple-element.23), channel_id=1, source_target_pairs={{1,0},{2,1},{3,2},{5,4},{6,5},{7,6},{9,8},{10,9},{11,10},{13,12},{... | collective-permute-start | bytes 786440 | tf_op jit(solution)/shard_map/ppermute | solution.py:15
  9.0 5.1 %copy-start.7 = (bf16[128,2,8,128]{3,2,1,0:T(8,128)(2,1)S(1)}, bf16[128,2,8,128]{3,2,1,0:T(8,128)(2,1)}, u32[]{:S(2)}) copy-start(bf16[128,2,8,128]{3,2,1,0:T(8,128)(2,1)} %param.7) | copy-start | bytes 1572868
  32.9 9.2 %collective-permute-start.2 = (f32[64,27,128]{2,0,1:T(8,128)}, f32[64,27,128]{2,0,1:T(8,128)}, u32[]{:S(2)}, u32[]{:S(2)}) collective-permute-start(f32[64,27,128]{2,0,1:T(8,128)} %constant_dynamic-slice_fusion.1), channel_id=1, source_target_pairs={{0,1},{1,0},{2,3},{3,2},{4,5},{5,4},{6,7},{7,6},{8,9},{9,8},{10,11... | collective-permute-start | bytes 2654216 | tf_op jit(solution)/shard_map/ppermute | solution.py:93
  35.4 16.0 %collective-permute-start.5 = (bf16[128,2,8,128]{3,0,2,1:T(8,128)(2,1)}, bf16[128,2,8,128]{3,0,2,1:T(8,128)(2,1)}, u32[]{:S(2)}, u32[]{:S(2)}) collective-permute-start(bf16[128,2,8,128]{3,0,2,1:T(8,128)(2,1)} %copy.20), channel_id=1, source_target_pairs={{4,0},{8,4},{12,8},{5,1},{9,5},{13,9},{6,2},{10,6},{14,10},{7,3},{... | collective-permute-start | bytes 1572872 | tf_op jit(solution)/shard_map/ppermute | solution.py:68
  36.7 16.0 %collective-permute-start.6 = (bf16[128,2,8,128]{3,0,2,1:T(8,128)(2,1)}, bf16[128,2,8,128]{3,0,2,1:T(8,128)(2,1)}, u32[]{:S(2)}, u32[]{:S(2)}) collective-permute-start(bf16[128,2,8,128]{3,0,2,1:T(8,128)(2,1)} %copy.20), channel_id=1, source_target_pairs={{0,4},{4,8},{8,12},{1,5},{5,9},{9,13},{2,6},{6,10},{10,14},{3,7},{... | collective-permute-start | bytes 1572872 | tf_op jit(solution)/shard_map/ppermute | solution.py:65
  44.6 24.1 %collective-permute-start.3 = (f32[64,27,128]{2,0,1:T(8,128)}, f32[64,27,128]{2,0,1:T(8,128)}, u32[]{:S(2)}, u32[]{:S(2)}) collective-permute-start(f32[64,27,128]{2,0,1:T(8,128)} %dynamic-slice_add_fusion.1), channel_id=1, source_target_pairs={{0,2},{1,3},{2,0},{3,1},{4,6},{5,7},{6,4},{7,5},{8,10},{9,11},{10,... | collective-permute-start | bytes 2654216 | tf_op jit(solution)/shard_map/ppermute | solution.py:96
  51.4 15.2 %collective-permute-start.9 = (bf16[128,2,8,128]{3,0,2,1:T(8,128)(2,1)}, bf16[128,2,8,128]{3,0,2,1:T(8,128)(2,1)}, u32[]{:S(2)}, u32[]{:S(2)}) collective-permute-start(bf16[128,2,8,128]{3,0,2,1:T(8,128)(2,1)} %collective-permute-done.5), channel_id=1, source_target_pairs={{4,0},{8,4},{5,1},{9,5},{6,2},{10,6},{7,3},{11,7},{20,16},{24,20},... | collective-permute-start | bytes 1572872 | tf_op jit(solution)/shard_map/ppermute | solution.py:68
  52.7 15.2 %collective-permute-start.7 = (bf16[128,2,8,128]{3,0,2,1:T(8,128)(2,1)}, bf16[128,2,8,128]{3,0,2,1:T(8,128)(2,1)}, u32[]{:S(2)}, u32[]{:S(2)}) collective-permute-start(bf16[128,2,8,128]{3,0,2,1:T(8,128)(2,1)} %collective-permute-done.6), channel_id=1, source_target_pairs={{4,8},{8,12},{5,9},{9,13},{6,10},{10,14},{7,11},{11,15},{20,24},{2... | collective-permute-start | bytes 1572872 | tf_op jit(solution)/shard_map/ppermute | solution.py:65
  66.6 14.3 %collective-permute-start.10 = (bf16[128,2,8,128]{3,0,2,1:T(8,128)(2,1)}, bf16[128,2,8,128]{3,0,2,1:T(8,128)(2,1)}, u32[]{:S(2)}, u32[]{:S(2)}) collective-permute-start(bf16[128,2,8,128]{3,0,2,1:T(8,128)(2,1)} %collective-permute-done.9), channel_id=1, source_target_pairs={{4,0},{5,1},{6,2},{7,3},{20,16},{21,17},{22,18},{23,19}} | collective-permute-start | bytes 1572872 | tf_op jit(solution)/shard_map/ppermute | solution.py:68
  67.9 14.0 %collective-permute-start.8 = (bf16[128,2,8,128]{3,0,2,1:T(8,128)(2,1)}, bf16[128,2,8,128]{3,0,2,1:T(8,128)(2,1)S(1)}, u32[]{:S(2)}, u32[]{:S(2)}) collective-permute-start(bf16[128,2,8,128]{3,0,2,1:T(8,128)(2,1)} %collective-permute-done.7), channel_id=1, source_target_pairs={{8,12},{9,13},{10,14},{11,15},{24,28},{25,29},{26,30},{27,31}} | collective-permute-start | bytes 1572872 | tf_op jit(solution)/shard_map/ppermute | solution.py:65
  70.2 14.1 %collective-permute-start.4 = (f32[64,27,128]{2,0,1:T(8,128)S(1)}, f32[64,27,128]{2,0,1:T(8,128)S(1)}, u32[]{:S(2)}, u32[]{:S(2)}) collective-permute-start(f32[64,27,128]{2,0,1:T(8,128)S(1)} %add.62), channel_id=1, source_target_pairs={{0,1},{1,0},{2,3},{3,2},{4,5},{5,4},{6,7},{7,6},{8,9},{9,8},{10,11... | collective-permute-start | bytes 2654216 | tf_op jit(solution)/shard_map/ppermute | solution.py:101
  84.4 16.0 %copy-start.4 = (bf16[512,2,8,128]{3,0,2,1:T(8,128)(2,1)}, bf16[512,2,8,128]{3,0,2,1:T(8,128)(2,1)S(1)}, u32[]{:S(2)}) copy-start(bf16[512,2,8,128]{3,0,2,1:T(8,128)(2,1)S(1)} %pad_maximum_fusion.1) | copy-start | bytes 6291460
  86.3 9.1 %collective-permute-start.12 = (bf16[512,1,8,128]{3,0,2,1:T(8,128)(2,1)S(1)}, bf16[512,1,8,128]{3,0,2,1:T(8,128)(2,1)S(1)}, u32[]{:S(2)}, u32[]{:S(2)}) collective-permute-start(bf16[512,1,8,128]{3,0,2,1:T(8,128)(2,1)S(1)} %get-tuple-element.19), channel_id=1, source_target_pairs={{1,0},{2,1},{3,2},{5,4},{6,5},{7,6},{9,8},{10,9},{11,10},{13,12},{... | collective-permute-start | bytes 3145736 | tf_op jit(solution)/shard_map/ppermute | solution.py:15
  87.6 12.8 %collective-permute-start.11 = (bf16[512,1,8,128]{3,0,2,1:T(8,128)(2,1)S(1)}, bf16[512,1,8,128]{3,0,2,1:T(8,128)(2,1)S(1)}, u32[]{:S(2)}, u32[]{:S(2)}) collective-permute-start(bf16[512,1,8,128]{3,0,2,1:T(8,128)(2,1)S(1)} %get-tuple-element.18), channel_id=1, source_target_pairs={{0,1},{1,2},{2,3},{4,5},{5,6},{6,7},{8,9},{9,10},{10,11},{12,13},{... | collective-permute-start | bytes 3145736 | tf_op jit(solution)/shard_map/ppermute | solution.py:12
  95.4 4.9 %copy-start.8 = (bf16[512,1,8,128]{3,0,2,1:T(8,128)(2,1)}, bf16[512,1,8,128]{3,0,2,1:T(8,128)(2,1)S(1)}, u32[]{:S(2)}) copy-start(bf16[512,1,8,128]{3,0,2,1:T(8,128)(2,1)S(1)} %collective-permute-done.12) | copy-start | bytes 3145732
  110.6 14.2 %collective-permute-start.13 = (f32[64,27,384]{2,0,1:T(8,128)}, f32[64,27,384]{2,0,1:T(8,128)}, u32[]{:S(2)}, u32[]{:S(2)}) collective-permute-start(f32[64,27,384]{2,0,1:T(8,128)} %constant_dynamic-slice_fusion), channel_id=1, source_target_pairs={{0,1},{1,0},{2,3},{3,2},{4,5},{5,4},{6,7},{7,6},{8,9},{9,8},{10,11... | collective-permute-start | bytes 7962632 | tf_op jit(solution)/shard_map/ppermute | solution.py:93
  119.2 5.5 %copy-start.3 = (f32[128,27,384]{2,0,1:T(8,128)S(1)}, f32[128,27,384]{2,0,1:T(8,128)}, u32[]{:S(2)}) copy-start(f32[128,27,384]{2,0,1:T(8,128)} %copy-done.2) | copy-start | bytes 15925252
  128.5 59.8 %collective-permute-start.14 = (f32[64,27,384]{2,0,1:T(8,128)}, f32[64,27,384]{2,0,1:T(8,128)}, u32[]{:S(2)}, u32[]{:S(2)}) collective-permute-start(f32[64,27,384]{2,0,1:T(8,128)} %dynamic-slice_add_fusion), channel_id=1, source_target_pairs={{0,2},{1,3},{2,0},{3,1},{4,6},{5,7},{6,4},{7,5},{8,10},{9,11},{10,... | collective-permute-start | bytes 7962632 | tf_op jit(solution)/shard_map/ppermute | solution.py:96
  140.8 17.2 %copy-start.10 = (f32[128]{0:T(128)S(1)}, f32[128]{0:T(128)}, u32[]{:S(2)}) copy-start(f32[128]{0:T(128)} %param.6) | copy-start | bytes 1540
  191.3 5.2 %collective-permute-start.15 = (f32[64,27,384]{2,0,1:T(8,128)S(1)}, f32[64,27,384]{2,0,1:T(8,128)}, u32[]{:S(2)}, u32[]{:S(2)}) collective-permute-start(f32[64,27,384]{2,0,1:T(8,128)S(1)} %add.71), channel_id=1, source_target_pairs={{0,1},{1,0},{2,3},{3,2},{4,5},{5,4},{6,7},{7,6},{8,9},{9,8},{10,11... | collective-permute-start | bytes 7962632 | tf_op jit(solution)/shard_map/ppermute | solution.py:101
  192.7 5.9 %copy-start.6 = (f32[128,27,128]{2,0,1:T(8,128)S(1)}, f32[128,27,128]{2,0,1:T(8,128)}, u32[]{:S(2)}) copy-start(f32[128,27,128]{2,0,1:T(8,128)} %pad_maximum_fusion.3) | copy-start | bytes 5308420
  198.6 4.6 %copy-start.1 = (bf16[128,27,512]{2,0,1:T(8,128)(2,1)S(1)}, bf16[128,27,512]{2,0,1:T(8,128)(2,1)}, u32[]{:S(2)}) copy-start(bf16[128,27,512]{2,0,1:T(8,128)(2,1)} %param.5) | copy-start | bytes 10616836
  (4 other events, 6.5 us)
